TPU v7x, 128 devices: a whole 4x4x4 slice. The times are simulated.
128 devices in a mesh: dp: 4 (over x), expert: 32 (over y, z, core).
Axes of the slice: x: 4, y: 4, z: 4, core: 2. Of those that a mesh axis runs over, the one named last changes fastest.
Arguments:
- tokens: bfloat16 [16384, 4096], P(('dp', 'expert')), may hold values from -6 to 6
- cotangent: bfloat16 [16384, 4096], P(('dp', 'expert')), may hold values from -6 to 6
- routes: int32 [16384], P(('dp', 'expert')), may hold values from 0 to 31, as said below
- combine: float32 [16384], P(('dp', 'expert')), may hold values from 0.05 to 1
- expert_weights: bfloat16 [32, 3, 1536, 4096], P('expert', None, 'dp'), may hold values from -0.09375 to 0.09375
Outputs:
- combined: bfloat16 [16384, 4096], P(('dp', 'expert'))
- token_grad: bfloat16 [16384, 4096], P(('dp', 'expert'))
- combine_grad: float32 [16384], P(('dp', 'expert'))
Inputs may be any that keep to these rules, and one draw needn't show every extreme that they name: `routes`: among the 128 rows of every device, two experts, the same two on every device, are each named by exactly 8 rows, and every other expert by 3 or 4 rows.
All inputs are finite; a program needn't handle non-finite values.
Results may differ from a plain program's by a relative error of at most 0.015.
Values may be sent and summed in bfloat16 or wider, within the bound.
No kernel may reach another device: no remote copies, remote signals or barrier semaphores. Data moves between devices by JAX's collectives and lax.ppermute only.
A program may use at most 192 MiB of HBM per device.

v0:
```python
import jax
import jax.numpy as jnp
from jax import lax
from jax.sharding import PartitionSpec as P


def placement(member, slot_count):
    within = jnp.sum((jnp.cumsum(member, 0) - 1) * member, 1)
    owner_group = jnp.sum(member * lax.iota(jnp.int32, member.shape[1])[None, :], 1)
    is_used = jnp.sum(member, 1) > 0
    target = owner_group * slot_count + within
    buffer_cells = lax.iota(jnp.int32, member.shape[1] * slot_count)
    return ((buffer_cells[:, None] == target[None, :]) & is_used[None, :]).astype(jnp.bfloat16)


def spread(layout, row_block):
    return jnp.dot(layout, row_block, preferred_element_type=jnp.float32).astype(jnp.bfloat16)


def collect(layout, buffer_rows):
    return lax.dot_general(
        layout, buffer_rows, (((0,), (0,)), ((), ())), preferred_element_type=jnp.float32
    )


def group_rows(values):
    return lax.all_gather(values, "dp", axis=0, tiled=True)


def group_sum(values):
    return lax.psum_scatter(
        values.astype(jnp.bfloat16), "dp", scatter_dimension=0, tiled=True
    ).astype(jnp.float32)


def send_rows(cold_buf, experts, slot_count, model_width):
    arrived = lax.all_to_all(
        cold_buf.reshape(experts, slot_count, model_width),
        "expert",
        split_axis=0,
        concat_axis=0,
        tiled=True,
    ).reshape(-1, model_width)
    cold_in = group_rows(arrived)
    hot_in = None
    return (cold_in, hot_in)


def return_rows(cold_part, experts, slot_count, model_width):
    cold_total = group_sum(cold_part)
    hot_out = None
    summed = cold_total.astype(jnp.bfloat16).reshape(experts, slot_count, model_width)
    cold_out = lax.all_to_all(summed, "expert", split_axis=0, concat_axis=0, tiled=True).reshape(
        -1, model_width
    )
    return (cold_out, hot_out)


def forward_rows(row_block, matrices):
    gate_up = jnp.einsum("rd,kfd->krf", row_block, matrices[:2], preferred_element_type=jnp.float32)
    gate_act = gate_up[0]
    up_act = gate_up[1]
    hidden = (gate_act * jax.nn.sigmoid(gate_act) * up_act).astype(jnp.bfloat16)
    partial_out = jnp.dot(hidden, matrices[2], preferred_element_type=jnp.float32)
    return (gate_act, up_act, partial_out)


def backward_rows(row_block, gate_act, up_act, matrices):
    hidden_grad = lax.dot_general(
        row_block, matrices[2], (((1,), (1,)), ((), ())), preferred_element_type=jnp.float32
    )
    squashed = jax.nn.sigmoid(gate_act)
    gate_grad = (hidden_grad * up_act * squashed * (1.0 + gate_act * (1.0 - squashed))).astype(
        jnp.bfloat16
    )
    up_grad = (hidden_grad * gate_act * squashed).astype(jnp.bfloat16)
    both_grads = jnp.stack([gate_grad, up_grad])
    return jnp.einsum("krf,kfd->rd", both_grads, matrices[:2], preferred_element_type=jnp.float32)


def shards(tokens, cotangent, routes, combine, expert_weights):
    weights = expert_weights[0]
    tok_dev = tokens.shape[0]
    model_width = tokens.shape[1]
    experts = lax.axis_size("expert")
    capacity = 2 * tok_dev // experts
    labels = lax.iota(jnp.int32, experts)
    member = (routes[:, None] == labels[None, :]).astype(jnp.int32)
    cold_layout = placement(member, capacity)
    cold_buf = spread(cold_layout, tokens)
    cold_in, hot_in = send_rows(cold_buf, experts, capacity, model_width)
    gate_act, up_act, cold_part = forward_rows(cold_in, weights)
    cold_out, hot_out = return_rows(cold_part, experts, capacity, model_width)
    expert_out = collect(cold_layout, cold_out)
    cotangent_wide = cotangent.astype(jnp.float32)
    combined = (combine[:, None] * expert_out).astype(jnp.bfloat16)
    combine_grad = jnp.sum(expert_out * cotangent_wide, 1)
    out_grad = (combine[:, None] * cotangent_wide).astype(jnp.bfloat16)
    cold_grad_buf = spread(cold_layout, out_grad)
    cold_grad_in, hot_grad_in = send_rows(cold_grad_buf, experts, capacity, model_width)
    cold_grad_part = backward_rows(cold_grad_in, gate_act, up_act, weights)
    cold_grad_out, hot_grad_out = return_rows(cold_grad_part, experts, capacity, model_width)
    input_grad = collect(cold_layout, cold_grad_out)
    token_grad = input_grad.astype(jnp.bfloat16)
    return (combined, token_grad, combine_grad)


def solution(mesh):
    return jax.shard_map(
        shards,
        mesh=mesh,
        in_specs=(
            P(("dp", "expert"), None),
            P(("dp", "expert"), None),
            P(("dp", "expert")),
            P(("dp", "expert")),
            P("expert", None, "dp", None),
        ),
        out_specs=(P(("dp", "expert"), None), P(("dp", "expert"), None), P(("dp", "expert"))),
        check_vma=False,
    )
```

profile of v0, /device:TPU:1, one launch (start us, length us, event | category | flops | bytes accessed | tf_op | source)
XLA Modules:
  0.0 446.6 jit_solution(15779998642776179402)
XLA Ops:
  7.2 0.0 copy-start
  7.2 0.0 all-gather.3.cloned.1.call-start
  7.2 0.8 fusion.49
  8.1 0.2 reduce_window_sum.11
  8.2 0.9 fusion.54
  9.1 0.0 copy-done
  9.1 0.7 fusion.6
  9.8 37.7 %all_to_all.20 = bf16[32,8,4096]{2,1,0:T(8,128)(2,1)} all-to-all(bf16[32,8,4096]{2,1,0:T(8,128)(2,1)S(1)} %fusion.6), channel_id=1, replica_groups=mesh['dp'=4,'expert'=32] {'expert'}, dimensions={0} | all-to-all | bytes 4194304 | tf_op jit(solution)/shard_map/all_to_all | solution.py:37
  47.5 0.0 copy-start.2
  47.5 0.0 copy-start.3
  47.5 0.0 all-gather.3.cloned.1.call-update
  47.5 0.0 all-gather.5.cloned.1.call-start
  47.6 1.1 copy-done.2
  48.7 0.0 copy-done.3
  48.7 0.8 fusion.7
  49.5 32.0 %all_to_all.21 = bf16[32,8,4096]{2,1,0:T(8,128)(2,1)} all-to-all(bf16[32,8,4096]{2,1,0:T(8,128)(2,1)S(1)} %fusion.7), channel_id=1, replica_groups=mesh['dp'=4,'expert'=32] {'expert'}, dimensions={0} | all-to-all | bytes 4194304 | tf_op jit(solution)/shard_map/all_to_all | solution.py:37
  81.5 0.0 all-gather.5.cloned.1.call-update
  81.5 0.0 reduce-scatter.5.cloned.1.call-start
  81.6 46.7 %all-gather.3.cloned.1.call-done = bf16[1024,4096]{1,0:T(8,128)(2,1)} async-done(((bf16[256,4096]{1,0:T(8,128)(2,1)}), bf16[1024,4096]{1,0:T(8,128)(2,1)}) %all-gather.3.cloned.1.call-update) | async-done | bytes 8388624 | tf_op jit(solution)/shard_map/all_gather | solution.py:27
  128.3 12.1 %fusion.18 = f32[2,1024,384]{2,1,0:T(8,128)} fusion(bf16[1,3,384,4096]{3,2,1,0:T(8,128)(2,1)} %param.9, bf16[1024,4096]{1,0:T(8,128)(2,1)} %all-gather.3.cloned.1.call-done), kind=kOutput, calls=%fused_computation.26 | convolution fusion | flops 6442450944 | bytes 17825792 | tf_op jit(solution)/shard_map/rd,kfd->krf/dot_general | solution.py:60
  140.5 73.6 %all-gather.5.cloned.1.call-done = bf16[1024,4096]{1,0:T(8,128)(2,1)} async-done(((bf16[256,4096]{1,0:T(8,128)(2,1)}), bf16[1024,4096]{1,0:T(8,128)(2,1)}) %all-gather.5.cloned.1.call-update) | async-done | bytes 8388624 | tf_op jit(solution)/shard_map/all_gather | solution.py:27
  214.1 10.1 %fusion.39 = (bf16[1,1024,384]{2,1,0:T(8,128)(2,1)S(1)}, bf16[1,1024,384]{2,1,0:T(8,128)(2,1)S(1)}) fusion(f32[2,1024,384]{2,1,0:T(8,128)} %fusion.18, bf16[1024,4096]{1,0:T(8,128)(2,1)} %all-gather.5.cloned.1.call-done, bf16[1,3,384,4096]{3,2,1,0:T(8,128)(2,1)} %param.9), kind=kOutput, calls=%fused_computation.47 | convolution fusion | flops 3226337280 | bytes 16252928 | tf_op jit(solution)/shard_map/dot_general | solution.py:69
  224.2 11.5 %bitcast_convert_fusion = bf16[1024,4096]{1,0:T(8,128)(2,1)} fusion(bf16[1,3,384,4096]{3,2,1,0:T(8,128)(2,1)} %param.9, bf16[1,1024,384]{2,1,0:T(8,128)(2,1)S(1)} %get-tuple-element.7, bf16[1,1024,384]{2,1,0:T(8,128)(2,1)S(1)} %get-tuple-element.6), kind=kOutput, calls=%fused_computation | convolution fusion | flops 6447431680 | bytes 16252928 | tf_op jit(solution)/shard_map/krf,kfd->rd/dot_general | solution.py:78
  235.7 0.0 reduce-scatter.5.cloned.1.call-update
  235.7 0.2 reduce-scatter.3.cloned.1.call-start
  235.9 11.0 %convolution_convert_fusion = bf16[1024,4096]{1,0:T(8,128)(2,1)} fusion(bf16[1,3,384,4096]{3,2,1,0:T(8,128)(2,1)} %param.9, f32[2,1024,384]{2,1,0:T(8,128)} %fusion.18), kind=kOutput, calls=%fused_computation.3 | convolution fusion | flops 3227779072 | bytes 14680064 | tf_op jit(solution)/shard_map/dot_general | solution.py:64
  246.9 0.0 reduce-scatter.3.cloned.1.call-update
  246.9 70.4 %reduce-scatter.5.cloned.1.call-done = bf16[256,4096]{1,0:T(8,128)(2,1)} async-done(((bf16[1024,4096]{1,0:T(8,128)(2,1)}), bf16[256,4096]{1,0:T(8,128)(2,1)}) %reduce-scatter.5.cloned.1.call-update) | async-done | bytes 2097168 | tf_op jit(solution)/shard_map/reduce_scatter | solution.py:31
  317.4 7.6 %all-to-all-start.3 = ((bf16[32,8,4096]{2,1,0:T(8,128)(2,1)}), bf16[32,8,4096]{2,1,0:T(8,128)(2,1)S(1)}, u32[]{:S(2)}, u32[]{:S(2)}) async-start(bf16[32,8,4096]{2,1,0:T(8,128)(2,1)} %bitcast.86), calls=%async_computation.5 | async-start | bytes 4194304 | tf_op jit(solution)/shard_map/all_to_all | solution.py:53
  325.0 74.9 %reduce-scatter.3.cloned.1.call-done = bf16[256,4096]{1,0:T(8,128)(2,1)} async-done(((bf16[1024,4096]{1,0:T(8,128)(2,1)}), bf16[256,4096]{1,0:T(8,128)(2,1)}) %reduce-scatter.3.cloned.1.call-update) | async-done | bytes 2097168 | tf_op jit(solution)/shard_map/reduce_scatter | solution.py:31
  399.9 0.0 all-to-all-done.3
  399.9 7.7 %all-to-all-start.1 = ((bf16[32,8,4096]{2,1,0:T(8,128)(2,1)}), bf16[32,8,4096]{2,1,0:T(8,128)(2,1)}, u32[]{:S(2)}, u32[]{:S(2)}) async-start(bf16[32,8,4096]{2,1,0:T(8,128)(2,1)} %bitcast.87), calls=%async_computation.2 | async-start | bytes 4194304 | tf_op jit(solution)/shard_map/all_to_all | solution.py:53
  407.6 0.0 copy-start.1
  407.6 1.5 convolution_convert_fusion.3
  409.1 26.9 %all-to-all-done.1 = bf16[32,8,4096]{2,1,0:T(8,128)(2,1)} async-done(((bf16[32,8,4096]{2,1,0:T(8,128)(2,1)}), bf16[32,8,4096]{2,1,0:T(8,128)(2,1)}, u32[]{:S(2)}, u32[]{:S(2)}) %all-to-all-start.1) | async-done | bytes 2097184 | tf_op jit(solution)/shard_map/all_to_all | solution.py:53
  436.0 4.1 fusion.14
  440.1 0.0 copy-done.1
  (2 shorter events, 0.0 us)
Async XLA Ops:
  7.2 2.0 copy-start
  7.2 121.1 %all-gather.3.cloned.1.call-start = ((), (), s32[]{:S(2)}) async-start(), calls=%async_computation.6 | async-start | bytes 10485760 | tf_op jit(solution)/shard_map/all_gather | solution.py:27
  47.5 1.2 copy-start.2
  47.5 1.2 copy-start.3
  47.5 166.6 %all-gather.5.cloned.1.call-start = ((), (), s32[]{:S(2)}) async-start(), calls=%async_computation.8 | async-start | bytes 10485760 | tf_op jit(solution)/shard_map/all_gather | solution.py:27
  81.5 235.8 %reduce-scatter.5.cloned.1.call-start = ((), (), s32[]{:S(2)}) async-start(), calls=%async_computation.9 | async-start | bytes 10485760 | tf_op jit(solution)/shard_map/reduce_scatter | solution.py:31
  235.7 164.2 %reduce-scatter.3.cloned.1.call-start = ((), (), s32[]{:S(2)}) async-start(), calls=%async_computation.7 | async-start | bytes 10485760 | tf_op jit(solution)/shard_map/reduce_scatter | solution.py:31
  317.4 82.6 %all-to-all-start.3 = ((bf16[32,8,4096]{2,1,0:T(8,128)(2,1)}), bf16[32,8,4096]{2,1,0:T(8,128)(2,1)S(1)}, u32[]{:S(2)}, u32[]{:S(2)}) async-start(bf16[32,8,4096]{2,1,0:T(8,128)(2,1)} %bitcast.86), calls=%async_computation.5 | async-start | bytes 4194304 | tf_op jit(solution)/shard_map/all_to_all | solution.py:53
  399.9 36.1 %all-to-all-start.1 = ((bf16[32,8,4096]{2,1,0:T(8,128)(2,1)}), bf16[32,8,4096]{2,1,0:T(8,128)(2,1)}, u32[]{:S(2)}, u32[]{:S(2)}) async-start(bf16[32,8,4096]{2,1,0:T(8,128)(2,1)} %bitcast.87), calls=%async_computation.2 | async-start | bytes 4194304 | tf_op jit(solution)/shard_map/all_to_all | solution.py:53
  407.6 32.4 %copy-start.1 = (bf16[128,4096]{1,0:T(8,128)(2,1)S(1)}, bf16[128,4096]{1,0:T(8,128)(2,1)}, u32[]{:S(2)}) copy-start(bf16[128,4096]{1,0:T(8,128)(2,1)} %param.5) | copy-start | bytes 3145732
Sparse Core Ops, SparseCore 0:
  47.6 80.6 all-gather.2
  130.0 84.0 all-gather.4
  235.8 81.4 reduce-scatter.4
  319.7 80.1 reduce-scatter.2
where the time goes:
time: 447 us
  waiting for transfers between devices  293 us (66%)
  blocking collectives  69.7 us (16%)
  matrix products  51.7 us (12%)
  starting transfers between devices  15.7 us (4%)
  between operations  13.9 us (3%)
    reduce_scatter x2, waiting for transfers between devices, group_sum(): lax.psum_scatter(values.astype(jnp.bfloat16), 'dp', scatter_dimension=0,...  145 us
    all_gather x2, waiting for transfers between devices, group_rows(): return lax.all_gather(values, 'dp', axis=0, tiled=True)  120 us
    all_to_all x2, blocking collectives, send_rows(): lax.all_to_all(cold_buf.reshape(experts, slot_count, model_width), 'exper...  69.7 us
    all_to_all x2, waiting for transfers between devices, return_rows(): lax.all_to_all(summed, 'expert', split_axis=0, concat_axis=0, tiled=True)  26.9 us
    all_to_all x2, starting transfers between devices, return_rows(): lax.all_to_all(summed, 'expert', split_axis=0, concat_axis=0, tiled=True)  15.3 us
    dot_general x1, matrix products, forward_rows(): jnp.einsum('rd,kfd->krf', row_block, matrices[:2], preferred_element_type...  12.1 us
    dot_general x1, matrix products, backward_rows(): jnp.einsum('krf,kfd->rd', both_grads, matrices[:2], preferred_element_typ...  11.5 us
    dot_general x1, matrix products, forward_rows(): jnp.dot(hidden, matrices[2], preferred_element_type=jnp.float32)  11 us
  transfers between devices with their start and end apart: 6, of which 5 were waited for; matrix products, arithmetic and copies ran while one was open for 6% of the time, Pallas kernels for 0%

commit v1 on v0

--- a/solution.py
+++ b/solution.py
@@ -30,30 +30,13 @@
 def group_sum(values):
     return lax.psum_scatter(
         values.astype(jnp.bfloat16), "dp", scatter_dimension=0, tiled=True
-    ).astype(jnp.float32)
+    )
 
 
-def send_rows(cold_buf, experts, slot_count, model_width):
-    arrived = lax.all_to_all(
-        cold_buf.reshape(experts, slot_count, model_width),
-        "expert",
-        split_axis=0,
-        concat_axis=0,
-        tiled=True,
+def exchange(rows, experts, model_width):
+    return lax.all_to_all(
+        rows.reshape(experts, -1, model_width), "expert", split_axis=0, concat_axis=0, tiled=True
     ).reshape(-1, model_width)
-    cold_in = group_rows(arrived)
-    hot_in = None
-    return (cold_in, hot_in)
-
-
-def return_rows(cold_part, experts, slot_count, model_width):
-    cold_total = group_sum(cold_part)
-    hot_out = None
-    summed = cold_total.astype(jnp.bfloat16).reshape(experts, slot_count, model_width)
-    cold_out = lax.all_to_all(summed, "expert", split_axis=0, concat_axis=0, tiled=True).reshape(
-        -1, model_width
-    )
-    return (cold_out, hot_out)
 
 
 def forward_rows(row_block, matrices):
@@ -84,23 +67,32 @@
     model_width = tokens.shape[1]
     experts = lax.axis_size("expert")
     capacity = 2 * tok_dev // experts
+    chunks = 2
+    chunk_slots = capacity // chunks
     labels = lax.iota(jnp.int32, experts)
     member = (routes[:, None] == labels[None, :]).astype(jnp.int32)
-    cold_layout = placement(member, capacity)
-    cold_buf = spread(cold_layout, tokens)
-    cold_in, hot_in = send_rows(cold_buf, experts, capacity, model_width)
-    gate_act, up_act, cold_part = forward_rows(cold_in, weights)
-    cold_out, hot_out = return_rows(cold_part, experts, capacity, model_width)
-    expert_out = collect(cold_layout, cold_out)
+    layout = placement(member, capacity).reshape(experts, capacity, tok_dev)
     cotangent_wide = cotangent.astype(jnp.float32)
+    out_grad = (combine[:, None] * cotangent_wide).astype(jnp.bfloat16)
+
+    layouts = [
+        layout[:, c * chunk_slots:(c + 1) * chunk_slots].reshape(-1, tok_dev) for c in range(chunks)
+    ]
+    tok_in = [group_rows(exchange(spread(lay, tokens), experts, model_width)) for lay in layouts]
+    cot_in = [group_rows(exchange(spread(lay, out_grad), experts, model_width)) for lay in layouts]
+    expert_out = None
+    input_grad = None
+    for c in range(chunks):
+        gate_act, up_act, part = forward_rows(tok_in[c], weights)
+        out_back = exchange(group_sum(part), experts, model_width)
+        piece = collect(layouts[c], out_back)
+        expert_out = piece if expert_out is None else expert_out + piece
+        grad_part = backward_rows(cot_in[c], gate_act, up_act, weights)
+        grad_back = exchange(group_sum(grad_part), experts, model_width)
+        piece = collect(layouts[c], grad_back)
+        input_grad = piece if input_grad is None else input_grad + piece
     combined = (combine[:, None] * expert_out).astype(jnp.bfloat16)
     combine_grad = jnp.sum(expert_out * cotangent_wide, 1)
-    out_grad = (combine[:, None] * cotangent_wide).astype(jnp.bfloat16)
-    cold_grad_buf = spread(cold_layout, out_grad)
-    cold_grad_in, hot_grad_in = send_rows(cold_grad_buf, experts, capacity, model_width)
-    cold_grad_part = backward_rows(cold_grad_in, gate_act, up_act, weights)
-    cold_grad_out, hot_grad_out = return_rows(cold_grad_part, experts, capacity, model_width)
-    input_grad = collect(cold_layout, cold_grad_out)
     token_grad = input_grad.astype(jnp.bfloat16)
     return (combined, token_grad, combine_grad)
 

time: 447 us -> 474 us (1.060)
  waiting for transfers between devices: 293 us -> 247 us
  matrix products: 51.7 us -> 70.8 us
  blocking collectives: 69.7 us -> 88.6 us
  local copies, waits for them, and re-layouts: 1.17 us -> 19.1 us
  starting transfers between devices: 15.7 us -> 31.2 us
    all_gather x2 -> x4, waiting for transfers between devices: 120 us -> 96.4 us  [group_rows(): return lax.all_gather(values, 'dp', axis=0, tiled=True)]
    all_to_all x2 -> x4, blocking collectives: 69.7 us -> 88.6 us  [exchange(): lax.all_to_all(rows.reshape(experts, -1, model_width), 'expert', split_ax...]
    reshape x0 -> x12, local copies, waits for them, and re-layouts: none -> 18 us  [the longest x8 12.6 us: exchange(): rows.reshape(experts, -1, model_width)]
    all_to_all x2 -> x4, starting transfers between devices: 15.3 us -> 30.7 us  [exchange(): lax.all_to_all(rows.reshape(experts, -1, model_width), 'expert', split_ax...]
    all_to_all x2 -> x4, waiting for transfers between devices: 26.9 us -> 11.9 us  [exchange(): lax.all_to_all(rows.reshape(experts, -1, model_width), 'expert', split_ax...]
    reduce_scatter x2 -> x4, waiting for transfers between devices: 145 us -> 138 us  [group_sum(): lax.psum_scatter(values.astype(jnp.bfloat16), 'dp', scatter_dimension=0,...]
    dot_general x1 -> x2, matrix products: 12.1 us -> 17.4 us  [forward_rows(): jnp.einsum('rd,kfd->krf', row_block, matrices[:2], preferred_element_type...]
    dot_general x2 -> x4, matrix products: 5.54 us -> 9.57 us  [collect(): lax.dot_general(layout, buffer_rows, (((0,), (0,)), ((), ())), preferred_...]
  transfers between devices with their start and end apart: 6 -> 12, of which waited for: 5 -> 8; matrix products, arithmetic and copies ran while one was open for 6% -> 17% of each run, Pallas kernels for 0% -> 0%
where the time goes in v1:
time: 474 us; the launch traced here: 473 us
  waiting for transfers between devices  247 us (52%)
  blocking collectives  88.6 us (19%)
  matrix products  70.8 us (15%)
  starting transfers between devices  31.2 us (7%)
  local copies, waits for them, and re-layouts  19.1 us (4%)
  between operations  14.4 us (3%)
    reduce_scatter x4, waiting for transfers between devices, group_sum(): lax.psum_scatter(values.astype(jnp.bfloat16), 'dp', scatter_dimension=0,...  138 us
    all_gather x4, waiting for transfers between devices, group_rows(): return lax.all_gather(values, 'dp', axis=0, tiled=True)  96.4 us
    all_to_all x4, blocking collectives, exchange(): lax.all_to_all(rows.reshape(experts, -1, model_width), 'expert', split_ax...  88.6 us
    all_to_all x4, starting transfers between devices, exchange(): lax.all_to_all(rows.reshape(experts, -1, model_width), 'expert', split_ax...  30.7 us
    dot_general x2, matrix products, forward_rows(): jnp.einsum('rd,kfd->krf', row_block, matrices[:2], preferred_element_type...  17.4 us
    dot_general x2, matrix products, backward_rows(): jnp.einsum('krf,kfd->rd', both_grads, matrices[:2], preferred_element_typ...  15.5 us
    dot_general x2, matrix products, forward_rows(): jnp.dot(hidden, matrices[2], preferred_element_type=jnp.float32)  13.5 us
    reshape x8, local copies, waits for them, and re-layouts, exchange(): rows.reshape(experts, -1, model_width)  12.6 us
  transfers between devices with their start and end apart: 12, of which 8 were waited for; matrix products, arithmetic and copies ran while one was open for 17% of the time, Pallas kernels for 0%

profile of v1, /device:TPU:1, one launch (start us, length us, event | category | flops | bytes accessed | tf_op | source)
XLA Modules:
  0.0 472.8 jit_solution(6738018536119864457)
XLA Ops:
  7.2 0.0 all-gather.7.cloned.1.call-start
  7.2 0.8 fusion.73
  8.1 0.2 reduce_window_sum.11
  8.2 0.9 fusion.74
  9.1 0.1 compare_and_fusion
  9.3 1.4 convolution_convert_fusion.4
  10.7 1.5 reshape.93
  12.2 26.4 %all_to_all.40 = bf16[32,4,4096]{2,1,0:T(4,128)(2,1)} all-to-all(bf16[32,4,4096]{2,1,0:T(4,128)(2,1)S(1)} %reshape.93), channel_id=1, replica_groups=mesh['dp'=4,'expert'=32] {'expert'}, dimensions={0} | all-to-all | bytes 2097152 | tf_op jit(solution)/shard_map/all_to_all | solution.py:37
  38.7 2.1 reshape.94
  40.8 0.0 all-gather.7.cloned.1.call-update
  40.8 0.0 all-gather.11.cloned.1.call-start
  40.9 0.5 convolution_convert_fusion.2
  41.4 1.2 reshape.99
  42.6 20.9 %all_to_all.41 = bf16[32,4,4096]{2,1,0:T(4,128)(2,1)S(1)} all-to-all(bf16[32,4,4096]{2,1,0:T(4,128)(2,1)} %reshape.99), channel_id=1, replica_groups=mesh['dp'=4,'expert'=32] {'expert'}, dimensions={0} | all-to-all | bytes 2097152 | tf_op jit(solution)/shard_map/all_to_all | solution.py:37
  63.5 1.1 reshape.100
  64.6 0.0 all-gather.11.cloned.1.call-update
  64.6 0.0 all-gather.5.cloned.1.call-start
  64.7 0.4 convolution_convert_fusion.5
  65.1 0.4 reshape.89
  65.6 20.7 %all_to_all.42 = bf16[32,4,4096]{2,1,0:T(4,128)(2,1)S(1)} all-to-all(bf16[32,4,4096]{2,1,0:T(4,128)(2,1)S(1)} %reshape.89), channel_id=1, replica_groups=mesh['dp'=4,'expert'=32] {'expert'}, dimensions={0} | all-to-all | bytes 2097152 | tf_op jit(solution)/shard_map/all_to_all | solution.py:37
  86.2 1.1 reshape.90
  87.3 0.0 all-gather.5.cloned.1.call-update
  87.3 0.0 all-gather.9.cloned.1.call-start
  87.4 0.5 convolution_convert_fusion.3
  87.9 0.4 reshape.96
  88.3 20.7 %all_to_all.43 = bf16[32,4,4096]{2,1,0:T(4,128)(2,1)S(1)} all-to-all(bf16[32,4,4096]{2,1,0:T(4,128)(2,1)S(1)} %reshape.96), channel_id=1, replica_groups=mesh['dp'=4,'expert'=32] {'expert'}, dimensions={0} | all-to-all | bytes 2097152 | tf_op jit(solution)/shard_map/all_to_all | solution.py:37
  109.0 1.1 reshape.97
  110.1 0.0 all-gather.9.cloned.1.call-update
  110.1 0.0 reduce-scatter.11.cloned.1.call-start
  110.2 0.0 all-gather.7.cloned.1.call-done
  110.2 8.8 %fusion.32 = f32[2,512,384]{2,1,0:T(8,128)} fusion(bf16[1,3,384,4096]{3,2,1,0:T(8,128)(2,1)} %param.9, bf16[512,4096]{1,0:T(8,128)(2,1)} %all-gather.7.cloned.1.call-done), kind=kOutput, calls=%fused_computation.43 | convolution fusion | flops 3221225472 | bytes 12058624 | tf_op jit(solution)/shard_map/rd,kfd->krf/dot_general | solution.py:43
  119.0 18.0 %all-gather.11.cloned.1.call-done = bf16[512,4096]{1,0:T(8,128)(2,1)} async-done(((bf16[128,4096]{1,0:T(8,128)(2,1)}), bf16[512,4096]{1,0:T(8,128)(2,1)}) %all-gather.11.cloned.1.call-update) | async-done | bytes 4194320 | tf_op jit(solution)/shard_map/all_gather | solution.py:27
  137.0 6.0 %fusion.72 = (bf16[1,512,384]{2,1,0:T(8,128)(2,1)S(1)}, bf16[1,512,384]{2,1,0:T(8,128)(2,1)S(1)}) fusion(f32[2,512,384]{2,1,0:T(8,128)} %fusion.32, bf16[512,4096]{1,0:T(8,128)(2,1)} %all-gather.11.cloned.1.call-done, bf16[1,3,384,4096]{3,2,1,0:T(8,128)(2,1)} %param.9), kind=kOutput, calls=%fused_computation.87 | convolution fusion | flops 1613168640 | bytes 9699328 | tf_op jit(solution)/shard_map/dot_general | solution.py:52
  143.0 7.7 %bitcast_convert_fusion = bf16[512,4096]{1,0:T(8,128)(2,1)} fusion(bf16[1,3,384,4096]{3,2,1,0:T(8,128)(2,1)} %param.9, bf16[1,512,384]{2,1,0:T(8,128)(2,1)S(1)} %get-tuple-element.9, bf16[1,512,384]{2,1,0:T(8,128)(2,1)S(1)} %get-tuple-element.8), kind=kOutput, calls=%fused_computation | convolution fusion | flops 3223715840 | bytes 11272192 | tf_op jit(solution)/shard_map/krf,kfd->rd/dot_general | solution.py:61
  150.8 0.0 reduce-scatter.11.cloned.1.call-update
  150.8 0.2 reduce-scatter.9.cloned.1.call-start
  151.0 36.9 %all-gather.5.cloned.1.call-done = bf16[512,4096]{1,0:T(8,128)(2,1)} async-done(((bf16[128,4096]{1,0:T(8,128)(2,1)}), bf16[512,4096]{1,0:T(8,128)(2,1)}) %all-gather.5.cloned.1.call-update) | async-done | bytes 4194320 | tf_op jit(solution)/shard_map/all_gather | solution.py:27
  187.9 8.7 %fusion.27 = f32[2,512,384]{2,1,0:T(8,128)} fusion(bf16[1,3,384,4096]{3,2,1,0:T(8,128)(2,1)} %param.9, bf16[512,4096]{1,0:T(8,128)(2,1)} %all-gather.5.cloned.1.call-done), kind=kOutput, calls=%fused_computation.42 | convolution fusion | flops 3221225472 | bytes 12058624 | tf_op jit(solution)/shard_map/rd,kfd->krf/dot_general | solution.py:43
  196.6 41.5 %all-gather.9.cloned.1.call-done = bf16[512,4096]{1,0:T(8,128)(2,1)} async-done(((bf16[128,4096]{1,0:T(8,128)(2,1)}), bf16[512,4096]{1,0:T(8,128)(2,1)}) %all-gather.9.cloned.1.call-update) | async-done | bytes 4194320 | tf_op jit(solution)/shard_map/all_gather | solution.py:27
  238.0 6.0 %fusion.71 = (bf16[1,512,384]{2,1,0:T(8,128)(2,1)S(1)}, bf16[1,512,384]{2,1,0:T(8,128)(2,1)S(1)}) fusion(f32[2,512,384]{2,1,0:T(8,128)} %fusion.27, bf16[512,4096]{1,0:T(8,128)(2,1)} %all-gather.9.cloned.1.call-done, bf16[1,3,384,4096]{3,2,1,0:T(8,128)(2,1)} %param.9), kind=kOutput, calls=%fused_computation.86 | convolution fusion | flops 1613168640 | bytes 9699328 | tf_op jit(solution)/shard_map/dot_general | solution.py:52
  244.0 7.7 %bitcast_convert_fusion.1 = bf16[512,4096]{1,0:T(8,128)(2,1)} fusion(bf16[1,3,384,4096]{3,2,1,0:T(8,128)(2,1)} %param.9, bf16[1,512,384]{2,1,0:T(8,128)(2,1)S(1)} %get-tuple-element.7, bf16[1,512,384]{2,1,0:T(8,128)(2,1)S(1)} %get-tuple-element.6), kind=kOutput, calls=%fused_computation.1 | convolution fusion | flops 3223715840 | bytes 11272192 | tf_op jit(solution)/shard_map/krf,kfd->rd/dot_general | solution.py:61
  251.8 0.0 reduce-scatter.9.cloned.1.call-update
  251.8 0.0 reduce-scatter.7.cloned.1.call-start
  251.8 6.7 %convolution_convert_fusion = bf16[512,4096]{1,0:T(8,128)(2,1)} fusion(bf16[1,3,384,4096]{3,2,1,0:T(8,128)(2,1)} %param.9, f32[2,512,384]{2,1,0:T(8,128)} %fusion.32), kind=kOutput, calls=%fused_computation.8 | convolution fusion | flops 1613889536 | bytes 8912896 | tf_op jit(solution)/shard_map/dot_general | solution.py:47
  258.6 0.0 reduce-scatter.5.cloned.1.call-start
  258.6 6.8 %convolution_convert_fusion.1 = bf16[512,4096]{1,0:T(8,128)(2,1)} fusion(bf16[1,3,384,4096]{3,2,1,0:T(8,128)(2,1)} %param.9, f32[2,512,384]{2,1,0:T(8,128)} %fusion.27), kind=kOutput, calls=%fused_computation.9 | convolution fusion | flops 1613889536 | bytes 8912896 | tf_op jit(solution)/shard_map/dot_general | solution.py:47
  265.5 22.0 %reduce-scatter.11.cloned.1.call-done = bf16[128,4096]{1,0:T(8,128)(2,1)} async-done(((bf16[512,4096]{1,0:T(8,128)(2,1)}), bf16[128,4096]{1,0:T(8,128)(2,1)}) %reduce-scatter.11.cloned.1.call-update) | async-done | bytes 1048592 | tf_op jit(solution)/shard_map/reduce_scatter | solution.py:31
  287.5 2.2 reshape.101
  289.7 7.6 %all-to-all-start.7 = ((bf16[32,4,4096]{2,1,0:T(4,128)(2,1)}), bf16[32,4,4096]{2,1,0:T(4,128)(2,1)S(1)}, u32[]{:S(2)}, u32[]{:S(2)}) async-start(bf16[32,4,4096]{2,1,0:T(4,128)(2,1)} %reshape.101), calls=%async_computation.11 | async-start | bytes 2097152 | tf_op jit(solution)/shard_map/all_to_all | solution.py:37
  297.4 39.1 %reduce-scatter.9.cloned.1.call-done = bf16[128,4096]{1,0:T(8,128)(2,1)} async-done(((bf16[512,4096]{1,0:T(8,128)(2,1)}), bf16[128,4096]{1,0:T(8,128)(2,1)}) %reduce-scatter.9.cloned.1.call-update) | async-done | bytes 1048592 | tf_op jit(solution)/shard_map/reduce_scatter | solution.py:31
  336.5 2.2 reshape.98
  338.7 7.7 %all-to-all-start.5 = ((bf16[32,4,4096]{2,1,0:T(4,128)(2,1)}), bf16[32,4,4096]{2,1,0:T(4,128)(2,1)S(1)}, u32[]{:S(2)}, u32[]{:S(2)}) async-start(bf16[32,4,4096]{2,1,0:T(4,128)(2,1)} %reshape.98), calls=%async_computation.8 | async-start | bytes 2097152 | tf_op jit(solution)/shard_map/all_to_all | solution.py:37
  346.4 39.0 %reduce-scatter.7.cloned.1.call-done = bf16[128,4096]{1,0:T(8,128)(2,1)} async-done(((bf16[512,4096]{1,0:T(8,128)(2,1)}), bf16[128,4096]{1,0:T(8,128)(2,1)}) %reduce-scatter.7.cloned.1.call-update) | async-done | bytes 1048592 | tf_op jit(solution)/shard_map/reduce_scatter | solution.py:31
  385.4 2.2 reshape.95
  387.6 1.0 copy-done.3
  388.7 7.7 %all-to-all-start.3 = ((bf16[32,4,4096]{2,1,0:T(4,128)(2,1)}), bf16[32,4,4096]{2,1,0:T(4,128)(2,1)S(1)}, u32[]{:S(2)}, u32[]{:S(2)}) async-start(bf16[32,4,4096]{2,1,0:T(4,128)(2,1)} %reshape.95), calls=%async_computation.5 | async-start | bytes 2097152 | tf_op jit(solution)/shard_map/all_to_all | solution.py:37
  396.3 38.2 %reduce-scatter.5.cloned.1.call-done = bf16[128,4096]{1,0:T(8,128)(2,1)} async-done(((bf16[512,4096]{1,0:T(8,128)(2,1)}), bf16[128,4096]{1,0:T(8,128)(2,1)}) %reduce-scatter.5.cloned.1.call-update) | async-done | bytes 1048592 | tf_op jit(solution)/shard_map/reduce_scatter | solution.py:31
  434.5 2.2 reshape.91
  436.8 7.7 %all-to-all-start.1 = ((bf16[32,4,4096]{2,1,0:T(4,128)(2,1)}), bf16[32,4,4096]{2,1,0:T(4,128)(2,1)}, u32[]{:S(2)}, u32[]{:S(2)}) async-start(bf16[32,4,4096]{2,1,0:T(4,128)(2,1)} %reshape.91), calls=%async_computation.2 | async-start | bytes 2097152 | tf_op jit(solution)/shard_map/all_to_all | solution.py:37
  444.5 0.9 convolution_bitcast_fusion
  445.4 2.2 convolution_bitcast_fusion.2
  447.6 1.9 fusion.8
  449.5 11.9 %all-to-all-done.1 = bf16[32,4,4096]{2,1,0:T(4,128)(2,1)} async-done(((bf16[32,4,4096]{2,1,0:T(4,128)(2,1)}), bf16[32,4,4096]{2,1,0:T(4,128)(2,1)}, u32[]{:S(2)}, u32[]{:S(2)}) %all-to-all-start.1) | async-done | bytes 1048608 | tf_op jit(solution)/shard_map/all_to_all | solution.py:37
  461.4 4.6 fusion.22
  (22 shorter events, 0.1 us)
Async XLA Ops:
  7.2 2.1 copy-start
  7.2 103.0 %all-gather.7.cloned.1.call-start = ((), (), s32[]{:S(2)}) async-start(), calls=%async_computation.14 | async-start | bytes 5242880 | tf_op jit(solution)/shard_map/all_gather | solution.py:27
  10.7 30.2 %copy-start.2 = (bf16[128,4096]{1,0:T(8,128)(2,1)S(1)}, bf16[128,4096]{1,0:T(8,128)(2,1)}, u32[]{:S(2)}) copy-start(bf16[128,4096]{1,0:T(8,128)(2,1)} %param.6) | copy-start | bytes 3145732
  10.7 30.2 %copy-start.5 = (f32[128]{0:T(128)S(1)}, f32[128]{0:T(128)}, u32[]{:S(2)}) copy-start(f32[128]{0:T(128)} %param.8) | copy-start | bytes 1540
  40.8 96.2 %all-gather.11.cloned.1.call-start = ((), (), s32[]{:S(2)}) async-start(), calls=%async_computation.18 | async-start | bytes 5242880 | tf_op jit(solution)/shard_map/all_gather | solution.py:27
  64.6 123.3 %all-gather.5.cloned.1.call-start = ((), (), s32[]{:S(2)}) async-start(), calls=%async_computation.12 | async-start | bytes 5242880 | tf_op jit(solution)/shard_map/all_gather | solution.py:27
  87.3 150.7 %all-gather.9.cloned.1.call-start = ((), (), s32[]{:S(2)}) async-start(), calls=%async_computation.16 | async-start | bytes 5242880 | tf_op jit(solution)/shard_map/all_gather | solution.py:27
  110.1 177.4 %reduce-scatter.11.cloned.1.call-start = ((), (), s32[]{:S(2)}) async-start(), calls=%async_computation.19 | async-start | bytes 5242880 | tf_op jit(solution)/shard_map/reduce_scatter | solution.py:31
  150.8 185.7 %reduce-scatter.9.cloned.1.call-start = ((), (), s32[]{:S(2)}) async-start(), calls=%async_computation.17 | async-start | bytes 5242880 | tf_op jit(solution)/shard_map/reduce_scatter | solution.py:31
  251.8 133.6 %reduce-scatter.7.cloned.1.call-start = ((), (), s32[]{:S(2)}) async-start(), calls=%async_computation.15 | async-start | bytes 5242880 | tf_op jit(solution)/shard_map/reduce_scatter | solution.py:31
  258.6 175.9 %reduce-scatter.5.cloned.1.call-start = ((), (), s32[]{:S(2)}) async-start(), calls=%async_computation.13 | async-start | bytes 5242880 | tf_op jit(solution)/shard_map/reduce_scatter | solution.py:31
  289.7 49.0 %all-to-all-start.7 = ((bf16[32,4,4096]{2,1,0:T(4,128)(2,1)}), bf16[32,4,4096]{2,1,0:T(4,128)(2,1)S(1)}, u32[]{:S(2)}, u32[]{:S(2)}) async-start(bf16[32,4,4096]{2,1,0:T(4,128)(2,1)} %reshape.101), calls=%async_computation.11 | async-start | bytes 2097152 | tf_op jit(solution)/shard_map/all_to_all | solution.py:37
  338.7 48.9 %all-to-all-start.5 = ((bf16[32,4,4096]{2,1,0:T(4,128)(2,1)}), bf16[32,4,4096]{2,1,0:T(4,128)(2,1)S(1)}, u32[]{:S(2)}, u32[]{:S(2)}) async-start(bf16[32,4,4096]{2,1,0:T(4,128)(2,1)} %reshape.98), calls=%async_computation.8 | async-start | bytes 2097152 | tf_op jit(solution)/shard_map/all_to_all | solution.py:37
  387.6 1.0 copy-start.3
  388.7 48.1 %all-to-all-start.3 = ((bf16[32,4,4096]{2,1,0:T(4,128)(2,1)}), bf16[32,4,4096]{2,1,0:T(4,128)(2,1)S(1)}, u32[]{:S(2)}, u32[]{:S(2)}) async-start(bf16[32,4,4096]{2,1,0:T(4,128)(2,1)} %reshape.95), calls=%async_computation.5 | async-start | bytes 2097152 | tf_op jit(solution)/shard_map/all_to_all | solution.py:37
  436.8 24.7 %all-to-all-start.1 = ((bf16[32,4,4096]{2,1,0:T(4,128)(2,1)}), bf16[32,4,4096]{2,1,0:T(4,128)(2,1)}, u32[]{:S(2)}, u32[]{:S(2)}) async-start(bf16[32,4,4096]{2,1,0:T(4,128)(2,1)} %reshape.91), calls=%async_computation.2 | async-start | bytes 2097152 | tf_op jit(solution)/shard_map/all_to_all | solution.py:37
  444.5 3.2 copy-start.4
  445.4 20.6 %copy-start.1 = (bf16[128,4096]{1,0:T(8,128)(2,1)S(1)}, bf16[128,4096]{1,0:T(8,128)(2,1)}, u32[]{:S(2)}) copy-start(bf16[128,4096]{1,0:T(8,128)(2,1)} %param.5) | copy-start | bytes 3145732
Sparse Core Ops, SparseCore 0:
  40.9 45.7 all-gather.6
  88.4 48.5 all-gather.10
  139.3 48.5 all-gather.4
  189.4 48.5 all-gather.8
  240.3 47.1 reduce-scatter.10
  289.9 46.5 reduce-scatter.8
  338.9 46.4 reduce-scatter.6
  387.9 46.5 reduce-scatter.4

commit v2 on v0

--- a/solution.py
+++ b/solution.py
@@ -90,14 +90,16 @@
     cold_buf = spread(cold_layout, tokens)
     cold_in, hot_in = send_rows(cold_buf, experts, capacity, model_width)
     gate_act, up_act, cold_part = forward_rows(cold_in, weights)
-    cold_out, hot_out = return_rows(cold_part, experts, capacity, model_width)
-    expert_out = collect(cold_layout, cold_out)
     cotangent_wide = cotangent.astype(jnp.float32)
-    combined = (combine[:, None] * expert_out).astype(jnp.bfloat16)
-    combine_grad = jnp.sum(expert_out * cotangent_wide, 1)
     out_grad = (combine[:, None] * cotangent_wide).astype(jnp.bfloat16)
     cold_grad_buf = spread(cold_layout, out_grad)
     cold_grad_in, hot_grad_in = send_rows(cold_grad_buf, experts, capacity, model_width)
+    cold_part = cold_part.astype(jnp.bfloat16)
+    cold_part, cold_grad_in = lax.optimization_barrier((cold_part, cold_grad_in))
+    cold_out, hot_out = return_rows(cold_part, experts, capacity, model_width)
+    expert_out = collect(cold_layout, cold_out)
+    combined = (combine[:, None] * expert_out).astype(jnp.bfloat16)
+    combine_grad = jnp.sum(expert_out * cotangent_wide, 1)
     cold_grad_part = backward_rows(cold_grad_in, gate_act, up_act, weights)
     cold_grad_out, hot_grad_out = return_rows(cold_grad_part, experts, capacity, model_width)
     input_grad = collect(cold_layout, cold_grad_out)

time: 447 us -> 427 us (0.955)
  waiting for transfers between devices: 293 us -> 273 us
    reduce_scatter x2, waiting for transfers between devices: 145 us -> 136 us  [group_sum(): lax.psum_scatter(values.astype(jnp.bfloat16), 'dp', scatter_dimension=0,...]
    all_gather x2, waiting for transfers between devices: 120 us -> 112 us  [group_rows(): return lax.all_gather(values, 'dp', axis=0, tiled=True)]
  transfers between devices with their start and end apart: 6 -> 6, of which waited for: 5 -> 5; matrix products, arithmetic and copies ran while one was open for 6% -> 11% of each run, Pallas kernels for 0% -> 0%
where the time goes in v2:
time: 427 us; the launch traced here: 426 us
  waiting for transfers between devices  273 us (64%)
  blocking collectives  69.7 us (16%)
  matrix products  49.6 us (12%)
  starting transfers between devices  15.7 us (4%)
  between operations  13.9 us (3%)
    reduce_scatter x2, waiting for transfers between devices, group_sum(): lax.psum_scatter(values.astype(jnp.bfloat16), 'dp', scatter_dimension=0,...  136 us
    all_gather x2, waiting for transfers between devices, group_rows(): return lax.all_gather(values, 'dp', axis=0, tiled=True)  112 us
    all_to_all x2, blocking collectives, send_rows(): lax.all_to_all(cold_buf.reshape(experts, slot_count, model_width), 'exper...  69.7 us
    all_to_all x2, waiting for transfers between devices, return_rows(): lax.all_to_all(summed, 'expert', split_axis=0, concat_axis=0, tiled=True)  24.7 us
    all_to_all x2, starting transfers between devices, return_rows(): lax.all_to_all(summed, 'expert', split_axis=0, concat_axis=0, tiled=True)  15.4 us
    dot_general x1, matrix products, backward_rows(): jnp.einsum('krf,kfd->rd', both_grads, matrices[:2], preferred_element_typ...  12.2 us
    dot_general x1, matrix products, forward_rows(): jnp.einsum('rd,kfd->krf', row_block, matrices[:2], preferred_element_type...  10.2 us
    dot_general x1, matrix products, backward_rows(): lax.dot_general(row_block, matrices[2], (((1,), (1,)), ((), ())), preferr...  10.1 us
  transfers between devices with their start and end apart: 6, of which 5 were waited for; matrix products, arithmetic and copies ran while one was open for 11% of the time, Pallas kernels for 0%

profile of v2, /device:TPU:1, one launch (start us, length us, event | category | flops | bytes accessed | tf_op | source)
XLA Modules:
  0.0 426.3 jit_solution(12102932333114516869)
XLA Ops:
  7.2 0.0 copy-start
  7.2 0.0 all-gather.3.cloned.1.call-start
  7.2 0.8 fusion.49
  8.1 0.2 reduce_window_sum.11
  8.2 0.9 fusion.54
  9.1 0.0 copy-done
  9.1 0.7 fusion.6
  9.8 37.7 %all_to_all.20 = bf16[32,8,4096]{2,1,0:T(8,128)(2,1)} all-to-all(bf16[32,8,4096]{2,1,0:T(8,128)(2,1)S(1)} %fusion.6), channel_id=1, replica_groups=mesh['dp'=4,'expert'=32] {'expert'}, dimensions={0} | all-to-all | bytes 4194304 | tf_op jit(solution)/shard_map/all_to_all | solution.py:37
  47.5 0.0 copy-start.2
  47.5 0.0 copy-start.3
  47.5 0.0 all-gather.3.cloned.1.call-update
  47.5 0.0 all-gather.5.cloned.1.call-start
  47.6 1.1 copy-done.2
  48.7 0.0 copy-done.3
  48.7 0.8 fusion.7
  49.5 32.0 %all_to_all.21 = bf16[32,8,4096]{2,1,0:T(8,128)(2,1)} all-to-all(bf16[32,8,4096]{2,1,0:T(8,128)(2,1)S(1)} %fusion.7), channel_id=1, replica_groups=mesh['dp'=4,'expert'=32] {'expert'}, dimensions={0} | all-to-all | bytes 4194304 | tf_op jit(solution)/shard_map/all_to_all | solution.py:37
  81.5 0.0 all-gather.5.cloned.1.call-update
  81.5 0.0 reduce-scatter.3.cloned.1.call-start
  81.6 46.7 %all-gather.3.cloned.1.call-done = bf16[1024,4096]{1,0:T(8,128)(2,1)} async-done(((bf16[256,4096]{1,0:T(8,128)(2,1)}), bf16[1024,4096]{1,0:T(8,128)(2,1)}) %all-gather.3.cloned.1.call-update) | async-done | bytes 8388624 | tf_op jit(solution)/shard_map/all_gather | solution.py:27
  128.3 10.2 %fusion.18 = f32[2,1024,384]{2,1,0:T(8,128)S(1)} fusion(bf16[1,3,384,4096]{3,2,1,0:T(8,128)(2,1)} %param.9, bf16[1024,4096]{1,0:T(8,128)(2,1)} %all-gather.3.cloned.1.call-done), kind=kOutput, calls=%fused_computation.26 | convolution fusion | flops 6442450944 | bytes 17825792 | tf_op jit(solution)/shard_map/rd,kfd->krf/dot_general | solution.py:60
  138.5 0.0 copy-start.4
  138.5 1.6 copy-done.4
  140.2 9.0 %convolution_convert_fusion = bf16[1024,4096]{1,0:T(8,128)(2,1)} fusion(bf16[1,3,384,4096]{3,2,1,0:T(8,128)(2,1)} %param.9, f32[2,1024,384]{2,1,0:T(8,128)S(1)} %fusion.18), kind=kOutput, calls=%fused_computation.3 | convolution fusion | flops 3227779072 | bytes 14680064 | tf_op jit(solution)/shard_map/dot_general | solution.py:64
  149.2 64.9 %all-gather.5.cloned.1.call-done = bf16[1024,4096]{1,0:T(8,128)(2,1)} async-done(((bf16[256,4096]{1,0:T(8,128)(2,1)}), bf16[1024,4096]{1,0:T(8,128)(2,1)}) %all-gather.5.cloned.1.call-update) | async-done | bytes 8388624 | tf_op jit(solution)/shard_map/all_gather | solution.py:27
  214.1 0.0 reduce-scatter.3.cloned.1.call-update
  214.1 0.2 reduce-scatter.5.cloned.1.call-start
  214.3 10.1 %fusion.39 = (bf16[1,1024,384]{2,1,0:T(8,128)(2,1)S(1)}, bf16[1,1024,384]{2,1,0:T(8,128)(2,1)S(1)}) fusion(f32[2,1024,384]{2,1,0:T(8,128)} %copy-done.4, bf16[1024,4096]{1,0:T(8,128)(2,1)} %all-gather.5.cloned.1.call-done, bf16[1,3,384,4096]{3,2,1,0:T(8,128)(2,1)} %param.9), kind=kOutput, calls=%fused_computation.47 | convolution fusion | flops 3226337280 | bytes 16252928 | tf_op jit(solution)/shard_map/dot_general | solution.py:69
  224.4 12.2 %bitcast_convert_fusion = bf16[1024,4096]{1,0:T(8,128)(2,1)} fusion(bf16[1,3,384,4096]{3,2,1,0:T(8,128)(2,1)} %param.9, bf16[1,1024,384]{2,1,0:T(8,128)(2,1)S(1)} %get-tuple-element.11, bf16[1,1024,384]{2,1,0:T(8,128)(2,1)S(1)} %get-tuple-element.10), kind=kOutput, calls=%fused_computation | convolution fusion | flops 6447431680 | bytes 16252928 | tf_op jit(solution)/shard_map/krf,kfd->rd/dot_general | solution.py:78
  236.6 0.0 reduce-scatter.5.cloned.1.call-update
  236.7 61.4 %reduce-scatter.3.cloned.1.call-done = bf16[256,4096]{1,0:T(8,128)(2,1)} async-done(((bf16[1024,4096]{1,0:T(8,128)(2,1)}), bf16[256,4096]{1,0:T(8,128)(2,1)}) %reduce-scatter.3.cloned.1.call-update) | async-done | bytes 2097168 | tf_op jit(solution)/shard_map/reduce_scatter | solution.py:31
  298.1 7.7 %all-to-all-start.2 = ((bf16[32,8,4096]{2,1,0:T(8,128)(2,1)}), bf16[32,8,4096]{2,1,0:T(8,128)(2,1)S(1)}, u32[]{:S(2)}, u32[]{:S(2)}) async-start(bf16[32,8,4096]{2,1,0:T(8,128)(2,1)} %bitcast.86), calls=%async_computation.3 | async-start | bytes 4194304 | tf_op jit(solution)/shard_map/all_to_all | solution.py:53
  305.8 74.9 %reduce-scatter.5.cloned.1.call-done = bf16[256,4096]{1,0:T(8,128)(2,1)} async-done(((bf16[1024,4096]{1,0:T(8,128)(2,1)}), bf16[256,4096]{1,0:T(8,128)(2,1)}) %reduce-scatter.5.cloned.1.call-update) | async-done | bytes 2097168 | tf_op jit(solution)/shard_map/reduce_scatter | solution.py:31
  380.7 0.0 all-to-all-done.2
  380.7 7.7 %all-to-all-start.3 = ((bf16[32,8,4096]{2,1,0:T(8,128)(2,1)}), bf16[32,8,4096]{2,1,0:T(8,128)(2,1)}, u32[]{:S(2)}, u32[]{:S(2)}) async-start(bf16[32,8,4096]{2,1,0:T(8,128)(2,1)} %bitcast.87), calls=%async_computation.5 | async-start | bytes 4194304 | tf_op jit(solution)/shard_map/all_to_all | solution.py:53
  388.4 0.0 copy-start.1
  388.4 3.6 fusion.14
  392.0 24.7 %all-to-all-done.3 = bf16[32,8,4096]{2,1,0:T(8,128)(2,1)} async-done(((bf16[32,8,4096]{2,1,0:T(8,128)(2,1)}), bf16[32,8,4096]{2,1,0:T(8,128)(2,1)}, u32[]{:S(2)}, u32[]{:S(2)}) %all-to-all-start.3) | async-done | bytes 2097184 | tf_op jit(solution)/shard_map/all_to_all | solution.py:53
  416.7 3.1 convolution_convert_fusion.3
  419.8 0.0 copy-done.1
  (2 shorter events, 0.0 us)
Async XLA Ops:
  7.2 2.0 copy-start
  7.2 121.1 %all-gather.3.cloned.1.call-start = ((), (), s32[]{:S(2)}) async-start(), calls=%async_computation.6 | async-start | bytes 10485760 | tf_op jit(solution)/shard_map/all_gather | solution.py:27
  47.5 1.2 copy-start.2
  47.5 1.2 copy-start.3
  47.5 166.6 %all-gather.5.cloned.1.call-start = ((), (), s32[]{:S(2)}) async-start(), calls=%async_computation.7 | async-start | bytes 10485760 | tf_op jit(solution)/shard_map/all_gather | solution.py:27
  81.5 216.6 %reduce-scatter.3.cloned.1.call-start = ((), (), s32[]{:S(2)}) async-start(), calls=%async_computation.8 | async-start | bytes 10485760 | tf_op jit(solution)/shard_map/reduce_scatter | solution.py:31
  138.5 1.6 copy-start.4
  214.1 166.5 %reduce-scatter.5.cloned.1.call-start = ((), (), s32[]{:S(2)}) async-start(), calls=%async_computation.9 | async-start | bytes 10485760 | tf_op jit(solution)/shard_map/reduce_scatter | solution.py:31
  298.1 82.6 %all-to-all-start.2 = ((bf16[32,8,4096]{2,1,0:T(8,128)(2,1)}), bf16[32,8,4096]{2,1,0:T(8,128)(2,1)S(1)}, u32[]{:S(2)}, u32[]{:S(2)}) async-start(bf16[32,8,4096]{2,1,0:T(8,128)(2,1)} %bitcast.86), calls=%async_computation.3 | async-start | bytes 4194304 | tf_op jit(solution)/shard_map/all_to_all | solution.py:53
  380.7 36.1 %all-to-all-start.3 = ((bf16[32,8,4096]{2,1,0:T(8,128)(2,1)}), bf16[32,8,4096]{2,1,0:T(8,128)(2,1)}, u32[]{:S(2)}, u32[]{:S(2)}) async-start(bf16[32,8,4096]{2,1,0:T(8,128)(2,1)} %bitcast.87), calls=%async_computation.5 | async-start | bytes 4194304 | tf_op jit(solution)/shard_map/all_to_all | solution.py:53
  388.4 31.4 %copy-start.1 = (bf16[128,4096]{1,0:T(8,128)(2,1)S(1)}, bf16[128,4096]{1,0:T(8,128)(2,1)}, u32[]{:S(2)}) copy-start(bf16[128,4096]{1,0:T(8,128)(2,1)} %param.5) | copy-start | bytes 3145732
Sparse Core Ops, SparseCore 0:
  47.6 80.6 all-gather.2
  130.0 84.0 all-gather.4
  216.6 81.4 reduce-scatter.2
  300.4 80.1 reduce-scatter.4

commit v3 on v2

--- a/solution.py
+++ b/solution.py
@@ -23,14 +23,32 @@
     )
 
 
+def shifted(values, step):
+    n = lax.axis_size("dp")
+    return lax.ppermute(values, "dp", perm=[(i, (i + step) % n) for i in range(n)])
+
+
 def group_rows(values):
-    return lax.all_gather(values, "dp", axis=0, tiled=True)
+    half = values.shape[0] // 2
+    from_left = shifted(values, 1)
+    from_right = shifted(values, -1)
+    far_head = shifted(from_left[:half], 1)
+    far_tail = shifted(from_right[half:], -1)
+    return jnp.concatenate([values, from_left, from_right, far_head, far_tail], 0)
 
 
 def group_sum(values):
-    return lax.psum_scatter(
-        values.astype(jnp.bfloat16), "dp", scatter_dimension=0, tiled=True
-    ).astype(jnp.float32)
+    own, to_left, to_right, far = jnp.split(values, 4, 0)
+    half = far.shape[0] // 2
+    far_head = shifted(far[:half].astype(jnp.bfloat16), -1).astype(jnp.float32)
+    far_tail = shifted(far[half:].astype(jnp.bfloat16), 1).astype(jnp.float32)
+    to_left = to_left.astype(jnp.bfloat16).astype(jnp.float32)
+    to_right = to_right.astype(jnp.bfloat16).astype(jnp.float32)
+    to_left = jnp.concatenate([to_left[:half] + far_head, to_left[half:]], 0)
+    to_right = jnp.concatenate([to_right[:half], to_right[half:] + far_tail], 0)
+    back_right = shifted(to_left.astype(jnp.bfloat16), -1).astype(jnp.float32)
+    back_left = shifted(to_right.astype(jnp.bfloat16), 1).astype(jnp.float32)
+    return own.astype(jnp.bfloat16).astype(jnp.float32) + back_right + back_left
 
 
 def send_rows(cold_buf, experts, slot_count, model_width):

time: 427 us -> 403 us (0.944)
  blocking collectives: 69.7 us -> 0 us
  starting transfers between devices: 15.7 us -> 54.1 us
  local copies, waits for them, and re-layouts: 2.81 us -> 17 us
  between operations: 13.9 us -> 0.94 us
  other arithmetic: 1.86 us -> 14.8 us
  waiting for transfers between devices: 273 us -> 268 us
    ppermute x0 -> x16, waiting for transfers between devices: none -> 189 us  [shifted(): lax.ppermute(values, 'dp', perm=[(i, (i + step) % n) for i in range(n)])]
    reduce_scatter x2 -> x0, waiting for transfers between devices: 136 us -> none  [group_sum(): lax.psum_scatter(values.astype(jnp.bfloat16), 'dp', scatter_dimension=0,...]
    all_gather x2 -> x0, waiting for transfers between devices: 112 us -> none  [group_rows(): return lax.all_gather(values, 'dp', axis=0, tiled=True)]
    all_to_all x2 -> x0, blocking collectives: 69.7 us -> none  [send_rows(): lax.all_to_all(cold_buf.reshape(experts, slot_count, model_width), 'exper...]
    all_to_all x0 -> x2, waiting for transfers between devices: none -> 51.8 us  [send_rows(): lax.all_to_all(cold_buf.reshape(experts, slot_count, model_width), 'exper...]
    ppermute x0 -> x16, starting transfers between devices: none -> 18.8 us  [shifted(): lax.ppermute(values, 'dp', perm=[(i, (i + step) % n) for i in range(n)])]
    all_to_all x0 -> x2, starting transfers between devices: none -> 14.3 us  [send_rows(): lax.all_to_all(cold_buf.reshape(experts, slot_count, model_width), 'exper...]
    unnamed x10 -> x20, local copies, waits for them, and re-layouts: 2.81 us -> 12.1 us
  transfers between devices with their start and end apart: 6 -> 20, of which waited for: 5 -> 14; matrix products, arithmetic and copies ran while one was open for 11% -> 12% of each run, Pallas kernels for 0% -> 0%
where the time goes in v3:
time: 403 us; the launch traced here: 402 us
  waiting for transfers between devices  268 us (67%)
  starting transfers between devices  54.1 us (13%)
  matrix products  47.4 us (12%)
  local copies, waits for them, and re-layouts  17 us (4%)
  other arithmetic  14.8 us (4%)
    ppermute x16, waiting for transfers between devices, shifted(): lax.ppermute(values, 'dp', perm=[(i, (i + step) % n) for i in range(n)])  189 us
    all_to_all x2, waiting for transfers between devices, send_rows(): lax.all_to_all(cold_buf.reshape(experts, slot_count, model_width), 'exper...  51.8 us
    all_to_all x2, waiting for transfers between devices, return_rows(): lax.all_to_all(summed, 'expert', split_axis=0, concat_axis=0, tiled=True)  26.9 us
    all_to_all x2, starting transfers between devices, return_rows(): lax.all_to_all(summed, 'expert', split_axis=0, concat_axis=0, tiled=True)  21.1 us
    ppermute x16, starting transfers between devices, shifted(): lax.ppermute(values, 'dp', perm=[(i, (i + step) % n) for i in range(n)])  18.8 us
    all_to_all x2, starting transfers between devices, send_rows(): lax.all_to_all(cold_buf.reshape(experts, slot_count, model_width), 'exper...  14.3 us
    unnamed x20, local copies, waits for them, and re-layouts  12.1 us
    dot_general x1, matrix products, backward_rows(): lax.dot_general(row_block, matrices[2], (((1,), (1,)), ((), ())), preferr...  11.3 us
  transfers between devices with their start and end apart: 20, of which 14 were waited for; matrix products, arithmetic and copies ran while one was open for 12% of the time, Pallas kernels for 0%

profile of v3, /device:TPU:1, one launch (start us, length us, event | category | flops | bytes accessed | tf_op | source)
XLA Modules:
  0.0 401.9 jit_solution(5768320918664947276)
XLA Ops:
  0.6 0.8 fusion.51
  1.5 0.2 reduce_window_sum.11
  1.7 0.9 fusion.56
  2.6 2.0 fusion.6
  4.6 9.7 %all-to-all-start = ((bf16[32,8,4096]{2,1,0:T(8,128)(2,1)}), bf16[32,8,4096]{2,1,0:T(8,128)(2,1)S(1)}, u32[]{:S(2)}, u32[]{:S(2)}) async-start(bf16[32,8,4096]{2,1,0:T(8,128)(2,1)} %fusion.6), calls=%async_computation | async-start | bytes 4194304 | tf_op jit(solution)/shard_map/all_to_all | solution.py:55
  14.3 2.2 fusion.7
  16.5 26.1 %all-to-all-done = bf16[32,8,4096]{2,1,0:T(8,128)(2,1)S(1)} async-done(((bf16[32,8,4096]{2,1,0:T(8,128)(2,1)}), bf16[32,8,4096]{2,1,0:T(8,128)(2,1)S(1)}, u32[]{:S(2)}, u32[]{:S(2)}) %all-to-all-start) | async-done | bytes 2097184 | tf_op jit(solution)/shard_map/all_to_all | solution.py:55
  42.6 1.3 copy-done.3
  43.9 4.5 %all-to-all-start.1 = ((bf16[32,8,4096]{2,1,0:T(8,128)(2,1)}), bf16[32,8,4096]{2,1,0:T(8,128)(2,1)S(1)}, u32[]{:S(2)}, u32[]{:S(2)}) async-start(bf16[32,8,4096]{2,1,0:T(8,128)(2,1)} %fusion.7), calls=%async_computation.1 | async-start | bytes 4194304 | tf_op jit(solution)/shard_map/all_to_all | solution.py:55
  48.5 1.3 collective-permute-start
  49.8 1.5 collective-permute-start.1
  51.2 25.6 %all-to-all-done.1 = bf16[32,8,4096]{2,1,0:T(8,128)(2,1)S(1)} async-done(((bf16[32,8,4096]{2,1,0:T(8,128)(2,1)}), bf16[32,8,4096]{2,1,0:T(8,128)(2,1)S(1)}, u32[]{:S(2)}, u32[]{:S(2)}) %all-to-all-start.1) | async-done | bytes 2097184 | tf_op jit(solution)/shard_map/all_to_all | solution.py:55
  76.9 1.2 collective-permute-start.4
  78.1 1.5 collective-permute-start.5
  79.5 1.7 constant_dynamic-update-slice_fusion.4
  81.3 1.5 constant_dynamic-update-slice_fusion.9
  82.8 14.1 %collective-permute-done = bf16[256,4096]{1,0:T(8,128)(2,1)} collective-permute-done((bf16[256,4096]{1,0:T(8,128)(2,1)}, bf16[256,4096]{1,0:T(8,128)(2,1)}, u32[]{:S(2)}, u32[]{:S(2)}) %collective-permute-start) | collective-permute-done | bytes 2097184 | tf_op jit(solution)/shard_map/ppermute | solution.py:28
  96.9 1.3 slice.121
  98.2 0.1 collective-permute-start.2
  98.3 1.3 slice.122
  99.6 2.7 collective-permute-start.3
  102.4 39.4 %collective-permute-done.4 = bf16[256,4096]{1,0:T(8,128)(2,1)S(1)} collective-permute-done((bf16[256,4096]{1,0:T(8,128)(2,1)S(1)}, bf16[256,4096]{1,0:T(8,128)(2,1)S(1)}, u32[]{:S(2)}, u32[]{:S(2)}) %collective-permute-start.4) | collective-permute-done | bytes 2097184 | tf_op jit(solution)/shard_map/ppermute | solution.py:28
  142.0 2.9 collective-permute-start.7
  144.9 1.7 constant_dynamic-update-slice_fusion.3
  146.7 1.7 constant_dynamic-update-slice_fusion.2
  148.4 1.5 constant_dynamic-update-slice_fusion.8
  149.9 1.5 constant_dynamic-update-slice_fusion.7
  151.3 12.9 %collective-permute-done.2 = bf16[128,4096]{1,0:T(8,128)(2,1)S(1)} collective-permute-done((bf16[128,4096]{1,0:T(8,128)(2,1)S(1)}, bf16[128,4096]{1,0:T(8,128)(2,1)S(1)}, u32[]{:S(2)}, u32[]{:S(2)}) %collective-permute-start.2) | collective-permute-done | bytes 1048608 | tf_op jit(solution)/shard_map/ppermute | solution.py:28
  164.4 10.9 %fusion.20 = f32[2,1024,384]{2,1,0:T(8,128)S(1)} fusion(bf16[1,3,384,4096]{3,2,1,0:T(8,128)(2,1)} %param.9, bf16[1024,4096]{1,0:T(8,128)(2,1)S(1)} %constant_dynamic-update-slice_fusion), kind=kOutput, calls=%fused_computation.38 | convolution fusion | flops 6442450944 | bytes 17825792 | tf_op jit(solution)/shard_map/rd,kfd->krf/dot_general | solution.py:78
  175.4 11.4 %collective-permute-done.6 = bf16[128,4096]{1,0:T(8,128)(2,1)S(1)} collective-permute-done((bf16[128,4096]{1,0:T(8,128)(2,1)S(1)}, bf16[128,4096]{1,0:T(8,128)(2,1)S(1)}, u32[]{:S(2)}, u32[]{:S(2)}) %collective-permute-start.6) | collective-permute-done | bytes 1048608 | tf_op jit(solution)/shard_map/ppermute | solution.py:28
  186.7 1.1 constant_dynamic-update-slice_fusion.6
  187.8 6.7 %convolution_convert_fusion = bf16[1024,4096]{1,0:T(8,128)(2,1)S(1)} fusion(bf16[1,3,384,4096]{3,2,1,0:T(8,128)(2,1)} %param.9, f32[2,1024,384]{2,1,0:T(8,128)S(1)} %fusion.20), kind=kOutput, calls=%fused_computation.3 | convolution fusion | flops 3227779072 | bytes 14680064 | tf_op jit(solution)/shard_map/dot_general | solution.py:82
  194.5 1.1 constant_dynamic-update-slice_fusion.5
  195.6 11.3 %fusion.41 = (bf16[1,1024,384]{2,1,0:T(8,128)(2,1)S(1)}, bf16[1,1024,384]{2,1,0:T(8,128)(2,1)S(1)}) fusion(f32[2,1024,384]{2,1,0:T(8,128)S(1)} %fusion.20, bf16[1024,4096]{1,0:T(8,128)(2,1)} %constant_dynamic-update-slice_fusion.5, bf16[1,3,384,4096]{3,2,1,0:T(8,128)(2,1)} %param.9), kind=kOutput, calls=%fused_computation.59 | convolution fusion | flops 3226337280 | bytes 16252928 | tf_op jit(solution)/shard_map/dot_general | solution.py:87
  206.9 8.8 %bitcast_convert_fusion = bf16[1024,4096]{1,0:T(8,128)(2,1)S(1)} fusion(bf16[1,3,384,4096]{3,2,1,0:T(8,128)(2,1)} %param.9, bf16[1,1024,384]{2,1,0:T(8,128)(2,1)S(1)} %get-tuple-element.23, bf16[1,1024,384]{2,1,0:T(8,128)(2,1)S(1)} %get-tuple-element.22), kind=kOutput, calls=%fused_computation | convolution fusion | flops 6447431680 | bytes 16252928 | tf_op jit(solution)/shard_map/krf,kfd->rd/dot_general | solution.py:96
  215.7 0.5 fusion.59
  216.2 1.6 collective-permute-start.12
  217.7 0.2 collective-permute-start.14
  217.9 0.5 fusion.60
  218.5 2.7 collective-permute-start.8
  221.2 18.8 %collective-permute-done.12 = bf16[128,4096]{1,0:T(8,128)(2,1)S(1)} collective-permute-done((bf16[128,4096]{1,0:T(8,128)(2,1)S(1)}, bf16[128,4096]{1,0:T(8,128)(2,1)S(1)}, u32[]{:S(2)}, u32[]{:S(2)}) %collective-permute-start.12) | collective-permute-done | bytes 1048608 | tf_op jit(solution)/shard_map/ppermute | solution.py:28
  240.0 2.2 collective-permute-done.14
  242.2 0.8 add_convert_fusion.3
  243.0 0.2 pad_maximum_fusion.2
  243.2 0.4 collective-permute-start.13
  243.5 0.2 pad_maximum_fusion.3
  243.7 1.3 collective-permute-start.15
  245.0 19.6 %collective-permute-done.10 = bf16[128,4096]{1,0:T(8,128)(2,1)S(1)} collective-permute-done((bf16[128,4096]{1,0:T(8,128)(2,1)S(1)}, bf16[128,4096]{1,0:T(8,128)(2,1)S(1)}, u32[]{:S(2)}, u32[]{:S(2)}) %collective-permute-start.10) | collective-permute-done | bytes 1048608 | tf_op jit(solution)/shard_map/ppermute | solution.py:28
  264.6 0.8 add_convert_fusion.5
  265.4 1.5 pad_maximum_fusion
  267.0 0.3 collective-permute-start.9
  267.2 1.5 pad_maximum_fusion.1
  268.8 1.2 collective-permute-start.11
  270.0 37.4 %collective-permute-done.13 = bf16[256,4096]{1,0:T(8,128)(2,1)S(1)} collective-permute-done((bf16[256,4096]{1,0:T(8,128)(2,1)S(1)}, bf16[256,4096]{1,0:T(8,128)(2,1)S(1)}, u32[]{:S(2)}, u32[]{:S(2)}) %collective-permute-start.13) | collective-permute-done | bytes 2097184 | tf_op jit(solution)/shard_map/ppermute | solution.py:28
  307.4 2.2 collective-permute-done.15
  309.6 2.5 fusion.16
  312.0 11.5 %all-to-all-start.3 = ((bf16[32,8,4096]{2,1,0:T(8,128)(2,1)}), bf16[32,8,4096]{2,1,0:T(8,128)(2,1)S(1)}, u32[]{:S(2)}, u32[]{:S(2)}) async-start(bf16[32,8,4096]{2,1,0:T(8,128)(2,1)} %fusion.16), calls=%async_computation.3 | async-start | bytes 4194304 | tf_op jit(solution)/shard_map/all_to_all | solution.py:71
  323.6 28.9 %collective-permute-done.9 = bf16[256,4096]{1,0:T(8,128)(2,1)} collective-permute-done((bf16[256,4096]{1,0:T(8,128)(2,1)}, bf16[256,4096]{1,0:T(8,128)(2,1)}, u32[]{:S(2)}, u32[]{:S(2)}) %collective-permute-start.9) | collective-permute-done | bytes 2097184 | tf_op jit(solution)/shard_map/ppermute | solution.py:28
  352.4 2.2 collective-permute-done.11
  354.6 5.3 %fusion.15 = bf16[32,8,4096]{2,1,0:T(8,128)(2,1)} fusion(bf16[256,4096]{1,0:T(8,128)(2,1)} %collective-permute-done.11, bf16[256,4096]{1,0:T(8,128)(2,1)} %collective-permute-done.9, bf16[1024,4096]{1,0:T(8,128)(2,1)} %copy-done.2), kind=kLoop, calls=%fused_computation.24 | loop fusion | flops 6291456 | bytes 8388608 | tf_op jit(solution)/shard_map/reshape | solution.py:70
  359.9 9.6 %all-to-all-start.2 = ((bf16[32,8,4096]{2,1,0:T(8,128)(2,1)}), bf16[32,8,4096]{2,1,0:T(8,128)(2,1)}, u32[]{:S(2)}, u32[]{:S(2)}) async-start(bf16[32,8,4096]{2,1,0:T(8,128)(2,1)} %fusion.15), calls=%async_computation.2 | async-start | bytes 4194304 | tf_op jit(solution)/shard_map/all_to_all | solution.py:71
  369.5 1.5 convolution_convert_fusion.3
  371.0 26.9 %all-to-all-done.2 = bf16[32,8,4096]{2,1,0:T(8,128)(2,1)} async-done(((bf16[32,8,4096]{2,1,0:T(8,128)(2,1)}), bf16[32,8,4096]{2,1,0:T(8,128)(2,1)}, u32[]{:S(2)}, u32[]{:S(2)}) %all-to-all-start.2) | async-done | bytes 2097184 | tf_op jit(solution)/shard_map/all_to_all | solution.py:71
  397.9 4.1 %fusion.14 = (f32[128]{0:T(128)}, bf16[128,4096]{1,0:T(8,128)(2,1)}) fusion(bf16[128,4096]{1,0:T(8,128)(2,1)} %param.6, f32[128]{0:T(128)S(1)} %copy-done.5, bf16[32,8,4096]{2,1,0:T(8,128)(2,1)} %all-to-all-done.2, s32[128]{0:T(128)S(1)} %multiply_add_fusion, pred[128]{0:T(512)(128)(4,1)S(1)} %broadcast_compare_fusion), kind=kOutput, calls=%fused_computation.23 | convolution fusion | flops 271122304 | bytes 4195968 | tf_op jit(solution)/shard_map/dot_general | solution.py:21
  (25 shorter events, 0.5 us)
Async XLA Ops:
  0.6 1.9 copy-start
  4.6 9.7 %copy-start.4 = (bf16[128,4096]{1,0:T(8,128)(2,1)S(1)}, bf16[128,4096]{1,0:T(8,128)(2,1)}, u32[]{:S(2)}) copy-start(bf16[128,4096]{1,0:T(8,128)(2,1)} %param.6) | copy-start | bytes 3145732
  4.6 9.7 %copy-start.5 = (f32[128]{0:T(128)S(1)}, f32[128]{0:T(128)}, u32[]{:S(2)}) copy-start(f32[128]{0:T(128)} %param.8) | copy-start | bytes 1540
  4.6 38.0 %all-to-all-start = ((bf16[32,8,4096]{2,1,0:T(8,128)(2,1)}), bf16[32,8,4096]{2,1,0:T(8,128)(2,1)S(1)}, u32[]{:S(2)}, u32[]{:S(2)}) async-start(bf16[32,8,4096]{2,1,0:T(8,128)(2,1)} %fusion.6), calls=%async_computation | async-start | bytes 4194304 | tf_op jit(solution)/shard_map/all_to_all | solution.py:55
  42.6 1.3 copy-start.3
  43.9 32.9 %all-to-all-start.1 = ((bf16[32,8,4096]{2,1,0:T(8,128)(2,1)}), bf16[32,8,4096]{2,1,0:T(8,128)(2,1)S(1)}, u32[]{:S(2)}, u32[]{:S(2)}) async-start(bf16[32,8,4096]{2,1,0:T(8,128)(2,1)} %fusion.7), calls=%async_computation.1 | async-start | bytes 4194304 | tf_op jit(solution)/shard_map/all_to_all | solution.py:55
  48.5 48.5 %collective-permute-start = (bf16[256,4096]{1,0:T(8,128)(2,1)}, bf16[256,4096]{1,0:T(8,128)(2,1)}, u32[]{:S(2)}, u32[]{:S(2)}) collective-permute-start(bf16[256,4096]{1,0:T(8,128)(2,1)} %bitcast.90), channel_id=1, source_target_pairs={{0,32},{32,64},{64,96},{96,0},{1,33},{33,65},{65,97},{97,1},{2,34}... | collective-permute-start | bytes 6291464 | tf_op jit(solution)/shard_map/ppermute | solution.py:28
  49.8 48.6 %collective-permute-start.1 = (bf16[256,4096]{1,0:T(8,128)(2,1)}, bf16[256,4096]{1,0:T(8,128)(2,1)}, u32[]{:S(2)}, u32[]{:S(2)}) collective-permute-start(bf16[256,4096]{1,0:T(8,128)(2,1)} %bitcast.91), channel_id=1, source_target_pairs={{0,96},{32,0},{64,32},{96,64},{1,97},{33,1},{65,33},{97,65},{2,98}... | collective-permute-start | bytes 6291464 | tf_op jit(solution)/shard_map/ppermute | solution.py:28
  76.9 64.9 %collective-permute-start.4 = (bf16[256,4096]{1,0:T(8,128)(2,1)S(1)}, bf16[256,4096]{1,0:T(8,128)(2,1)S(1)}, u32[]{:S(2)}, u32[]{:S(2)}) collective-permute-start(bf16[256,4096]{1,0:T(8,128)(2,1)S(1)} %bitcast.88), channel_id=1, source_target_pairs={{0,32},{32,64},{64,96},{96,0},{1,33},{33,65},{65,97},{97,1},{2,34}... | collective-permute-start | bytes 6291464 | tf_op jit(solution)/shard_map/ppermute | solution.py:28
  78.1 63.9 %collective-permute-start.5 = (bf16[256,4096]{1,0:T(8,128)(2,1)S(1)}, bf16[256,4096]{1,0:T(8,128)(2,1)S(1)}, u32[]{:S(2)}, u32[]{:S(2)}) collective-permute-start(bf16[256,4096]{1,0:T(8,128)(2,1)S(1)} %bitcast.89), channel_id=1, source_target_pairs={{0,96},{32,0},{64,32},{96,64},{1,97},{33,1},{65,33},{97,65},{2,98}... | collective-permute-start | bytes 6291464 | tf_op jit(solution)/shard_map/ppermute | solution.py:28
  98.2 66.0 %collective-permute-start.2 = (bf16[128,4096]{1,0:T(8,128)(2,1)S(1)}, bf16[128,4096]{1,0:T(8,128)(2,1)S(1)}, u32[]{:S(2)}, u32[]{:S(2)}) collective-permute-start(bf16[128,4096]{1,0:T(8,128)(2,1)S(1)} %slice.121), channel_id=1, source_target_pairs={{0,32},{32,64},{64,96},{96,0},{1,33},{33,65},{65,97},{97,1},{2,34}... | collective-permute-start | bytes 3145736 | tf_op jit(solution)/shard_map/ppermute | solution.py:28
  99.6 64.7 %collective-permute-start.3 = (bf16[128,4096]{1,0:T(8,128)(2,1)S(1)}, bf16[128,4096]{1,0:T(8,128)(2,1)S(1)}, u32[]{:S(2)}, u32[]{:S(2)}) collective-permute-start(bf16[128,4096]{1,0:T(8,128)(2,1)S(1)} %slice.122), channel_id=1, source_target_pairs={{0,96},{32,0},{64,32},{96,64},{1,97},{33,1},{65,33},{97,65},{2,98}... | collective-permute-start | bytes 3145736 | tf_op jit(solution)/shard_map/ppermute | solution.py:28
  141.9 44.9 %collective-permute-start.6 = (bf16[128,4096]{1,0:T(8,128)(2,1)S(1)}, bf16[128,4096]{1,0:T(8,128)(2,1)S(1)}, u32[]{:S(2)}, u32[]{:S(2)}) collective-permute-start(bf16[128,4096]{1,0:T(8,128)(2,1)S(1)} %slice.125), channel_id=1, source_target_pairs={{0,32},{32,64},{64,96},{96,0},{1,33},{33,65},{65,97},{97,1},{2,34}... | collective-permute-start | bytes 3145736 | tf_op jit(solution)/shard_map/ppermute | solution.py:28
  142.0 52.4 %collective-permute-start.7 = (bf16[128,4096]{1,0:T(8,128)(2,1)S(1)}, bf16[128,4096]{1,0:T(8,128)(2,1)S(1)}, u32[]{:S(2)}, u32[]{:S(2)}) collective-permute-start(bf16[128,4096]{1,0:T(8,128)(2,1)S(1)} %slice.126), channel_id=1, source_target_pairs={{0,96},{32,0},{64,32},{96,64},{1,97},{33,1},{65,33},{97,65},{2,98}... | collective-permute-start | bytes 3145736 | tf_op jit(solution)/shard_map/ppermute | solution.py:28
  194.4 70.2 %copy-start.2 = (bf16[1024,4096]{1,0:T(8,128)(2,1)}, bf16[1024,4096]{1,0:T(8,128)(2,1)S(1)}, u32[]{:S(2)}) copy-start(bf16[1024,4096]{1,0:T(8,128)(2,1)S(1)} %convolution_convert_fusion) | copy-start | bytes 25165828
  216.2 23.8 %collective-permute-start.12 = (bf16[128,4096]{1,0:T(8,128)(2,1)S(1)}, bf16[128,4096]{1,0:T(8,128)(2,1)S(1)}, u32[]{:S(2)}, u32[]{:S(2)}) collective-permute-start(bf16[128,4096]{1,0:T(8,128)(2,1)S(1)} %get-tuple-element.12), channel_id=1, source_target_pairs={{0,96},{32,0},{64,32},{96,64},{1,97},{33,1},{65,33},{97,65},{2,98}... | collective-permute-start | bytes 3145736 | tf_op jit(solution)/shard_map/ppermute | solution.py:28
  217.7 24.4 %collective-permute-start.14 = (bf16[128,4096]{1,0:T(8,128)(2,1)S(1)}, bf16[128,4096]{1,0:T(8,128)(2,1)S(1)}, u32[]{:S(2)}, u32[]{:S(2)}) collective-permute-start(bf16[128,4096]{1,0:T(8,128)(2,1)S(1)} %get-tuple-element.13), channel_id=1, source_target_pairs={{0,32},{32,64},{64,96},{96,0},{1,33},{33,65},{65,97},{97,1},{2,34}... | collective-permute-start | bytes 3145736 | tf_op jit(solution)/shard_map/ppermute | solution.py:28
  218.4 46.2 %collective-permute-start.10 = (bf16[128,4096]{1,0:T(8,128)(2,1)S(1)}, bf16[128,4096]{1,0:T(8,128)(2,1)S(1)}, u32[]{:S(2)}, u32[]{:S(2)}) collective-permute-start(bf16[128,4096]{1,0:T(8,128)(2,1)S(1)} %get-tuple-element.19), channel_id=1, source_target_pairs={{0,32},{32,64},{64,96},{96,0},{1,33},{33,65},{65,97},{97,1},{2,34}... | collective-permute-start | bytes 3145736 | tf_op jit(solution)/shard_map/ppermute | solution.py:28
  218.5 46.1 %collective-permute-start.8 = (bf16[128,4096]{1,0:T(8,128)(2,1)S(1)}, bf16[128,4096]{1,0:T(8,128)(2,1)S(1)}, u32[]{:S(2)}, u32[]{:S(2)}) collective-permute-start(bf16[128,4096]{1,0:T(8,128)(2,1)S(1)} %get-tuple-element.18), channel_id=1, source_target_pairs={{0,96},{32,0},{64,32},{96,64},{1,97},{33,1},{65,33},{97,65},{2,98}... | collective-permute-start | bytes 3145736 | tf_op jit(solution)/shard_map/ppermute | solution.py:28
  243.2 64.2 %collective-permute-start.13 = (bf16[256,4096]{1,0:T(8,128)(2,1)S(1)}, bf16[256,4096]{1,0:T(8,128)(2,1)S(1)}, u32[]{:S(2)}, u32[]{:S(2)}) collective-permute-start(bf16[256,4096]{1,0:T(8,128)(2,1)S(1)} %pad_maximum_fusion.2), channel_id=1, source_target_pairs={{0,96},{32,0},{64,32},{96,64},{1,97},{33,1},{65,33},{97,65},{2,98}... | collective-permute-start | bytes 6291464 | tf_op jit(solution)/shard_map/ppermute | solution.py:28
  243.7 65.8 %collective-permute-start.15 = (bf16[256,4096]{1,0:T(8,128)(2,1)S(1)}, bf16[256,4096]{1,0:T(8,128)(2,1)S(1)}, u32[]{:S(2)}, u32[]{:S(2)}) collective-permute-start(bf16[256,4096]{1,0:T(8,128)(2,1)S(1)} %pad_maximum_fusion.3), channel_id=1, source_target_pairs={{0,32},{32,64},{64,96},{96,0},{1,33},{33,65},{65,97},{97,1},{2,34}... | collective-permute-start | bytes 6291464 | tf_op jit(solution)/shard_map/ppermute | solution.py:28
  267.0 85.4 %collective-permute-start.9 = (bf16[256,4096]{1,0:T(8,128)(2,1)}, bf16[256,4096]{1,0:T(8,128)(2,1)}, u32[]{:S(2)}, u32[]{:S(2)}) collective-permute-start(bf16[256,4096]{1,0:T(8,128)(2,1)} %pad_maximum_fusion), channel_id=1, source_target_pairs={{0,96},{32,0},{64,32},{96,64},{1,97},{33,1},{65,33},{97,65},{2,98}... | collective-permute-start | bytes 6291464 | tf_op jit(solution)/shard_map/ppermute | solution.py:28
  268.8 85.8 %collective-permute-start.11 = (bf16[256,4096]{1,0:T(8,128)(2,1)}, bf16[256,4096]{1,0:T(8,128)(2,1)}, u32[]{:S(2)}, u32[]{:S(2)}) collective-permute-start(bf16[256,4096]{1,0:T(8,128)(2,1)} %pad_maximum_fusion.1), channel_id=1, source_target_pairs={{0,32},{32,64},{64,96},{96,0},{1,33},{33,65},{65,97},{97,1},{2,34}... | collective-permute-start | bytes 6291464 | tf_op jit(solution)/shard_map/ppermute | solution.py:28
  312.0 47.9 %all-to-all-start.3 = ((bf16[32,8,4096]{2,1,0:T(8,128)(2,1)}), bf16[32,8,4096]{2,1,0:T(8,128)(2,1)S(1)}, u32[]{:S(2)}, u32[]{:S(2)}) async-start(bf16[32,8,4096]{2,1,0:T(8,128)(2,1)} %fusion.16), calls=%async_computation.3 | async-start | bytes 4194304 | tf_op jit(solution)/shard_map/all_to_all | solution.py:71
  359.9 37.9 %all-to-all-start.2 = ((bf16[32,8,4096]{2,1,0:T(8,128)(2,1)}), bf16[32,8,4096]{2,1,0:T(8,128)(2,1)}, u32[]{:S(2)}, u32[]{:S(2)}) async-start(bf16[32,8,4096]{2,1,0:T(8,128)(2,1)} %fusion.15), calls=%async_computation.2 | async-start | bytes 4194304 | tf_op jit(solution)/shard_map/all_to_all | solution.py:71
  369.5 32.4 %copy-start.1 = (bf16[128,4096]{1,0:T(8,128)(2,1)S(1)}, bf16[128,4096]{1,0:T(8,128)(2,1)}, u32[]{:S(2)}) copy-start(bf16[128,4096]{1,0:T(8,128)(2,1)} %param.5) | copy-start | bytes 3145732

commit v4 on v3

--- a/solution.py
+++ b/solution.py
@@ -51,17 +51,14 @@
     return own.astype(jnp.bfloat16).astype(jnp.float32) + back_right + back_left
 
 
-def send_rows(cold_buf, experts, slot_count, model_width):
-    arrived = lax.all_to_all(
+def arrive_rows(cold_buf, experts, slot_count, model_width):
+    return lax.all_to_all(
         cold_buf.reshape(experts, slot_count, model_width),
         "expert",
         split_axis=0,
         concat_axis=0,
         tiled=True,
     ).reshape(-1, model_width)
-    cold_in = group_rows(arrived)
-    hot_in = None
-    return (cold_in, hot_in)
 
 
 def return_rows(cold_part, experts, slot_count, model_width):
@@ -106,12 +103,14 @@
     member = (routes[:, None] == labels[None, :]).astype(jnp.int32)
     cold_layout = placement(member, capacity)
     cold_buf = spread(cold_layout, tokens)
-    cold_in, hot_in = send_rows(cold_buf, experts, capacity, model_width)
-    gate_act, up_act, cold_part = forward_rows(cold_in, weights)
+    cold_in = group_rows(arrive_rows(cold_buf, experts, capacity, model_width))
     cotangent_wide = cotangent.astype(jnp.float32)
     out_grad = (combine[:, None] * cotangent_wide).astype(jnp.bfloat16)
     cold_grad_buf = spread(cold_layout, out_grad)
-    cold_grad_in, hot_grad_in = send_rows(cold_grad_buf, experts, capacity, model_width)
+    cold_grad_arrived = arrive_rows(cold_grad_buf, experts, capacity, model_width)
+    cold_grad_arrived, cold_in = lax.optimization_barrier((cold_grad_arrived, cold_in))
+    gate_act, up_act, cold_part = forward_rows(cold_in, weights)
+    cold_grad_in = group_rows(cold_grad_arrived)
     cold_part = cold_part.astype(jnp.bfloat16)
     cold_part, cold_grad_in = lax.optimization_barrier((cold_part, cold_grad_in))
     cold_out, hot_out = return_rows(cold_part, experts, capacity, model_width)

time: 403 us -> 392 us (0.973)
  blocking collectives: 0 us -> 37.8 us
  waiting for transfers between devices: 268 us -> 233 us
  matrix products: 47.4 us -> 41 us
  starting transfers between devices: 54.1 us -> 49 us
    all_to_all x2 -> x1, waiting for transfers between devices: 51.8 us -> 0.01 us  [arrive_rows(): lax.all_to_all(cold_buf.reshape(experts, slot_count, model_width), 'exper...]
    all_to_all x0 -> x1, blocking collectives: none -> 37.8 us  [arrive_rows(): lax.all_to_all(cold_buf.reshape(experts, slot_count, model_width), 'exper...]
    ppermute x16, waiting for transfers between devices: 189 us -> 206 us  [shifted(): lax.ppermute(values, 'dp', perm=[(i, (i + step) % n) for i in range(n)])]
    all_to_all x2 -> x1, starting transfers between devices: 14.3 us -> 4.51 us  [arrive_rows(): lax.all_to_all(cold_buf.reshape(experts, slot_count, model_width), 'exper...]
    dot_general x1, matrix products: 11.3 us -> 6.93 us  [backward_rows(): lax.dot_general(row_block, matrices[2], (((1,), (1,)), ((), ())), preferr...]
    unnamed x20 -> x18, local copies, waits for them, and re-layouts: 12.1 us -> 11.1 us
  transfers between devices with their start and end apart: 20 -> 19, of which waited for: 14 -> 13; matrix products, arithmetic and copies ran while one was open for 12% -> 12% of each run, Pallas kernels for 0% -> 0%
where the time goes in v4:
time: 392 us
  waiting for transfers between devices  233 us (59%)
  starting transfers between devices  49 us (12%)
  matrix products  41 us (10%)
  blocking collectives  37.8 us (10%)
  local copies, waits for them, and re-layouts  15.5 us (4%)
  other arithmetic  14.5 us (4%)
    ppermute x16, waiting for transfers between devices, shifted(): lax.ppermute(values, 'dp', perm=[(i, (i + step) % n) for i in range(n)])  206 us
    all_to_all x1, blocking collectives, arrive_rows(): lax.all_to_all(cold_buf.reshape(experts, slot_count, model_width), 'exper...  37.8 us
    all_to_all x2, waiting for transfers between devices, return_rows(): lax.all_to_all(summed, 'expert', split_axis=0, concat_axis=0, tiled=True)  26.9 us
    all_to_all x2, starting transfers between devices, return_rows(): lax.all_to_all(summed, 'expert', split_axis=0, concat_axis=0, tiled=True)  23.9 us
    ppermute x16, starting transfers between devices, shifted(): lax.ppermute(values, 'dp', perm=[(i, (i + step) % n) for i in range(n)])  20.6 us
    unnamed x18, local copies, waits for them, and re-layouts  11.1 us
    dot_general x1, matrix products, forward_rows(): jnp.einsum('rd,kfd->krf', row_block, matrices[:2], preferred_element_type...  10.2 us
    dot_general x1, matrix products, backward_rows(): jnp.einsum('krf,kfd->rd', both_grads, matrices[:2], preferred_element_typ...  8.78 us
  transfers between devices with their start and end apart: 19, of which 13 were waited for; matrix products, arithmetic and copies ran while one was open for 12% of the time, Pallas kernels for 0%

profile of v4, /device:TPU:1, one launch (start us, length us, event | category | flops | bytes accessed | tf_op | source)
XLA Modules:
  0.0 391.6 jit_solution(12010476123159751687)
XLA Ops:
  0.6 0.8 fusion.51
  1.5 0.2 reduce_window_sum.11
  1.7 0.9 fusion.56
  2.6 0.7 fusion.7
  3.3 37.8 %all_to_all.20 = bf16[32,8,4096]{2,1,0:T(8,128)(2,1)} all-to-all(bf16[32,8,4096]{2,1,0:T(8,128)(2,1)S(1)} %fusion.7), channel_id=1, replica_groups=mesh['dp'=4,'expert'=32] {'expert'}, dimensions={0} | all-to-all | bytes 4194304 | tf_op jit(solution)/shard_map/all_to_all | solution.py:55
  41.1 1.2 collective-permute-start
  42.3 1.5 collective-permute-start.1
  43.7 2.2 fusion.6
  45.9 4.5 %all-to-all-start = ((bf16[32,8,4096]{2,1,0:T(8,128)(2,1)}), bf16[32,8,4096]{2,1,0:T(8,128)(2,1)S(1)}, u32[]{:S(2)}, u32[]{:S(2)}) async-start(bf16[32,8,4096]{2,1,0:T(8,128)(2,1)} %fusion.6), calls=%async_computation | async-start | bytes 4194304 | tf_op jit(solution)/shard_map/all_to_all | solution.py:55
  50.4 39.2 %collective-permute-done = bf16[256,4096]{1,0:T(8,128)(2,1)} collective-permute-done((bf16[256,4096]{1,0:T(8,128)(2,1)}, bf16[256,4096]{1,0:T(8,128)(2,1)}, u32[]{:S(2)}, u32[]{:S(2)}) %collective-permute-start) | collective-permute-done | bytes 2097184 | tf_op jit(solution)/shard_map/ppermute | solution.py:28
  89.7 1.3 slice.121
  91.1 3.2 constant_dynamic-update-slice_fusion.4
  94.2 1.3 slice.122
  95.5 2.7 collective-permute-start.3
  98.3 3.1 constant_dynamic-update-slice_fusion.3
  101.4 3.2 constant_dynamic-update-slice_fusion.2
  104.5 11.4 %collective-permute-done.2 = bf16[128,4096]{1,0:T(8,128)(2,1)S(1)} collective-permute-done((bf16[128,4096]{1,0:T(8,128)(2,1)S(1)}, bf16[128,4096]{1,0:T(8,128)(2,1)S(1)}, u32[]{:S(2)}, u32[]{:S(2)}) %collective-permute-start.2) | collective-permute-done | bytes 1048608 | tf_op jit(solution)/shard_map/ppermute | solution.py:28
  116.0 1.1 constant_dynamic-update-slice_fusion.1
  117.0 2.4 collective-permute-done.3
  119.5 1.1 constant_dynamic-update-slice_fusion
  120.6 0.7 collective-permute-start.4
  121.3 2.7 collective-permute-start.5
  124.0 10.2 %fusion.20 = f32[2,1024,384]{2,1,0:T(8,128)S(1)} fusion(bf16[1,3,384,4096]{3,2,1,0:T(8,128)(2,1)} %param.9, bf16[1024,4096]{1,0:T(8,128)(2,1)} %constant_dynamic-update-slice_fusion), kind=kOutput, calls=%fused_computation.38 | convolution fusion | flops 6442450944 | bytes 17825792 | tf_op jit(solution)/shard_map/rd,kfd->krf/dot_general | solution.py:75
  134.2 6.7 %convolution_convert_fusion = bf16[1024,4096]{1,0:T(8,128)(2,1)S(1)} fusion(bf16[1,3,384,4096]{3,2,1,0:T(8,128)(2,1)} %param.9, f32[2,1024,384]{2,1,0:T(8,128)S(1)} %fusion.20), kind=kOutput, calls=%fused_computation.3 | convolution fusion | flops 3227779072 | bytes 14680064 | tf_op jit(solution)/shard_map/dot_general | solution.py:79
  140.9 26.9 %collective-permute-done.4 = bf16[256,4096]{1,0:T(8,128)(2,1)S(1)} collective-permute-done((bf16[256,4096]{1,0:T(8,128)(2,1)S(1)}, bf16[256,4096]{1,0:T(8,128)(2,1)S(1)}, u32[]{:S(2)}, u32[]{:S(2)}) %collective-permute-start.4) | collective-permute-done | bytes 2097184 | tf_op jit(solution)/shard_map/ppermute | solution.py:28
  167.8 0.1 slice.125
  167.9 0.1 collective-permute-start.6
  168.0 0.1 constant_dynamic-update-slice_fusion.9
  168.2 2.9 collective-permute-start.7
  171.1 0.1 constant_dynamic-update-slice_fusion.8
  171.3 0.1 constant_dynamic-update-slice_fusion.7
  171.4 19.6 %collective-permute-done.6 = bf16[128,4096]{1,0:T(8,128)(2,1)S(1)} collective-permute-done((bf16[128,4096]{1,0:T(8,128)(2,1)S(1)}, bf16[128,4096]{1,0:T(8,128)(2,1)S(1)}, u32[]{:S(2)}, u32[]{:S(2)}) %collective-permute-start.6) | collective-permute-done | bytes 1048608 | tf_op jit(solution)/shard_map/ppermute | solution.py:28
  191.0 0.1 constant_dynamic-update-slice_fusion.6
  191.1 0.1 constant_dynamic-update-slice_fusion.5
  191.2 6.9 %fusion.41 = (bf16[1,1024,384]{2,1,0:T(8,128)(2,1)S(1)}, bf16[1,1024,384]{2,1,0:T(8,128)(2,1)S(1)}) fusion(f32[2,1024,384]{2,1,0:T(8,128)S(1)} %fusion.20, bf16[1024,4096]{1,0:T(8,128)(2,1)S(1)} %constant_dynamic-update-slice_fusion.5, bf16[1,3,384,4096]{3,2,1,0:T(8,128)(2,1)} %param.9), kind=kOutput, calls=%fused_computation.59 | convolution fusion | flops 3226337280 | bytes 16252928 | tf_op jit(solution)/shard_map/dot_general | solution.py:84
  198.1 8.8 %bitcast_convert_fusion = bf16[1024,4096]{1,0:T(8,128)(2,1)S(1)} fusion(bf16[1,3,384,4096]{3,2,1,0:T(8,128)(2,1)} %param.9, bf16[1,1024,384]{2,1,0:T(8,128)(2,1)S(1)} %get-tuple-element.27, bf16[1,1024,384]{2,1,0:T(8,128)(2,1)S(1)} %get-tuple-element.26), kind=kOutput, calls=%fused_computation | convolution fusion | flops 6447431680 | bytes 16252928 | tf_op jit(solution)/shard_map/krf,kfd->rd/dot_general | solution.py:93
  206.9 0.3 fusion.59
  207.2 2.8 collective-permute-start.12
  210.1 0.3 fusion.60
  210.4 2.7 collective-permute-start.8
  213.2 15.3 %collective-permute-done.12 = bf16[128,4096]{1,0:T(8,128)(2,1)S(1)} collective-permute-done((bf16[128,4096]{1,0:T(8,128)(2,1)S(1)}, bf16[128,4096]{1,0:T(8,128)(2,1)S(1)}, u32[]{:S(2)}, u32[]{:S(2)}) %collective-permute-start.12) | collective-permute-done | bytes 1048608 | tf_op jit(solution)/shard_map/ppermute | solution.py:28
  228.5 3.1 collective-permute-done.14
  231.6 0.7 add_convert_fusion.3
  232.3 0.2 pad_maximum_fusion.2
  232.6 0.4 collective-permute-start.13
  232.9 0.2 pad_maximum_fusion.3
  233.1 1.2 collective-permute-start.15
  234.4 19.7 %collective-permute-done.10 = bf16[128,4096]{1,0:T(8,128)(2,1)S(1)} collective-permute-done((bf16[128,4096]{1,0:T(8,128)(2,1)S(1)}, bf16[128,4096]{1,0:T(8,128)(2,1)S(1)}, u32[]{:S(2)}, u32[]{:S(2)}) %collective-permute-start.10) | collective-permute-done | bytes 1048608 | tf_op jit(solution)/shard_map/ppermute | solution.py:28
  254.1 0.7 add_convert_fusion.5
  254.8 1.5 pad_maximum_fusion
  256.3 0.3 collective-permute-start.9
  256.6 1.6 pad_maximum_fusion.1
  258.2 1.2 collective-permute-start.11
  259.4 36.6 %collective-permute-done.13 = bf16[256,4096]{1,0:T(8,128)(2,1)S(1)} collective-permute-done((bf16[256,4096]{1,0:T(8,128)(2,1)S(1)}, bf16[256,4096]{1,0:T(8,128)(2,1)S(1)}, u32[]{:S(2)}, u32[]{:S(2)}) %collective-permute-start.13) | collective-permute-done | bytes 2097184 | tf_op jit(solution)/shard_map/ppermute | solution.py:28
  295.9 3.1 collective-permute-done.15
  299.0 2.4 fusion.16
  301.5 14.1 %all-to-all-start.3 = ((bf16[32,8,4096]{2,1,0:T(8,128)(2,1)}), bf16[32,8,4096]{2,1,0:T(8,128)(2,1)S(1)}, u32[]{:S(2)}, u32[]{:S(2)}) async-start(bf16[32,8,4096]{2,1,0:T(8,128)(2,1)} %fusion.16), calls=%async_computation.3 | async-start | bytes 4194304 | tf_op jit(solution)/shard_map/all_to_all | solution.py:68
  315.6 25.3 %collective-permute-done.9 = bf16[256,4096]{1,0:T(8,128)(2,1)} collective-permute-done((bf16[256,4096]{1,0:T(8,128)(2,1)}, bf16[256,4096]{1,0:T(8,128)(2,1)}, u32[]{:S(2)}, u32[]{:S(2)}) %collective-permute-start.9) | collective-permute-done | bytes 2097184 | tf_op jit(solution)/shard_map/ppermute | solution.py:28
  341.0 3.1 collective-permute-done.11
  344.1 5.3 %fusion.15 = bf16[32,8,4096]{2,1,0:T(8,128)(2,1)} fusion(bf16[256,4096]{1,0:T(8,128)(2,1)} %collective-permute-done.11, bf16[256,4096]{1,0:T(8,128)(2,1)} %collective-permute-done.9, bf16[1024,4096]{1,0:T(8,128)(2,1)} %copy-done.2), kind=kLoop, calls=%fused_computation.24 | loop fusion | flops 6291456 | bytes 8388608 | tf_op jit(solution)/shard_map/reshape | solution.py:67
  349.4 9.8 %all-to-all-start.2 = ((bf16[32,8,4096]{2,1,0:T(8,128)(2,1)}), bf16[32,8,4096]{2,1,0:T(8,128)(2,1)}, u32[]{:S(2)}, u32[]{:S(2)}) async-start(bf16[32,8,4096]{2,1,0:T(8,128)(2,1)} %fusion.15), calls=%async_computation.2 | async-start | bytes 4194304 | tf_op jit(solution)/shard_map/all_to_all | solution.py:68
  359.2 1.5 convolution_convert_fusion.3
  360.6 26.9 %all-to-all-done.2 = bf16[32,8,4096]{2,1,0:T(8,128)(2,1)} async-done(((bf16[32,8,4096]{2,1,0:T(8,128)(2,1)}), bf16[32,8,4096]{2,1,0:T(8,128)(2,1)}, u32[]{:S(2)}, u32[]{:S(2)}) %all-to-all-start.2) | async-done | bytes 2097184 | tf_op jit(solution)/shard_map/all_to_all | solution.py:68
  387.5 4.1 %fusion.14 = (f32[128]{0:T(128)}, bf16[128,4096]{1,0:T(8,128)(2,1)}) fusion(bf16[128,4096]{1,0:T(8,128)(2,1)} %param.6, f32[128]{0:T(128)S(1)} %copy-done.4, bf16[32,8,4096]{2,1,0:T(8,128)(2,1)} %all-to-all-done.2, s32[128]{0:T(128)S(1)} %multiply_add_fusion, pred[128]{0:T(512)(128)(4,1)S(1)} %broadcast_compare_fusion), kind=kOutput, calls=%fused_computation.23 | convolution fusion | flops 271122304 | bytes 4195968 | tf_op jit(solution)/shard_map/dot_general | solution.py:21
  (22 shorter events, 0.3 us)
Async XLA Ops:
  0.6 1.9 copy-start
  3.3 40.5 %copy-start.3 = (bf16[128,4096]{1,0:T(8,128)(2,1)S(1)}, bf16[128,4096]{1,0:T(8,128)(2,1)}, u32[]{:S(2)}) copy-start(bf16[128,4096]{1,0:T(8,128)(2,1)} %param.6) | copy-start | bytes 3145732
  3.3 40.5 %copy-start.4 = (f32[128]{0:T(128)S(1)}, f32[128]{0:T(128)}, u32[]{:S(2)}) copy-start(f32[128]{0:T(128)} %param.8) | copy-start | bytes 1540
  41.1 48.6 %collective-permute-start = (bf16[256,4096]{1,0:T(8,128)(2,1)}, bf16[256,4096]{1,0:T(8,128)(2,1)}, u32[]{:S(2)}, u32[]{:S(2)}) collective-permute-start(bf16[256,4096]{1,0:T(8,128)(2,1)} %bitcast.3), channel_id=1, source_target_pairs={{0,32},{32,64},{64,96},{96,0},{1,33},{33,65},{65,97},{97,1},{2,34}... | collective-permute-start | bytes 6291464 | tf_op jit(solution)/shard_map/ppermute | solution.py:28
  42.3 51.9 %collective-permute-start.1 = (bf16[256,4096]{1,0:T(8,128)(2,1)}, bf16[256,4096]{1,0:T(8,128)(2,1)}, u32[]{:S(2)}, u32[]{:S(2)}) collective-permute-start(bf16[256,4096]{1,0:T(8,128)(2,1)} %bitcast.3), channel_id=1, source_target_pairs={{0,96},{32,0},{64,32},{96,64},{1,97},{33,1},{65,33},{97,65},{2,98}... | collective-permute-start | bytes 6291464 | tf_op jit(solution)/shard_map/ppermute | solution.py:28
  45.9 74.7 %all-to-all-start = ((bf16[32,8,4096]{2,1,0:T(8,128)(2,1)}), bf16[32,8,4096]{2,1,0:T(8,128)(2,1)S(1)}, u32[]{:S(2)}, u32[]{:S(2)}) async-start(bf16[32,8,4096]{2,1,0:T(8,128)(2,1)} %fusion.6), calls=%async_computation | async-start | bytes 4194304 | tf_op jit(solution)/shard_map/all_to_all | solution.py:55
  91.0 25.0 %collective-permute-start.2 = (bf16[128,4096]{1,0:T(8,128)(2,1)S(1)}, bf16[128,4096]{1,0:T(8,128)(2,1)S(1)}, u32[]{:S(2)}, u32[]{:S(2)}) collective-permute-start(bf16[128,4096]{1,0:T(8,128)(2,1)S(1)} %slice.121), channel_id=1, source_target_pairs={{0,32},{32,64},{64,96},{96,0},{1,33},{33,65},{65,97},{97,1},{2,34}... | collective-permute-start | bytes 3145736 | tf_op jit(solution)/shard_map/ppermute | solution.py:28
  95.5 23.9 %collective-permute-start.3 = (bf16[128,4096]{1,0:T(8,128)(2,1)S(1)}, bf16[128,4096]{1,0:T(8,128)(2,1)S(1)}, u32[]{:S(2)}, u32[]{:S(2)}) collective-permute-start(bf16[128,4096]{1,0:T(8,128)(2,1)S(1)} %slice.122), channel_id=1, source_target_pairs={{0,96},{32,0},{64,32},{96,64},{1,97},{33,1},{65,33},{97,65},{2,98}... | collective-permute-start | bytes 3145736 | tf_op jit(solution)/shard_map/ppermute | solution.py:28
  120.6 47.2 %collective-permute-start.4 = (bf16[256,4096]{1,0:T(8,128)(2,1)S(1)}, bf16[256,4096]{1,0:T(8,128)(2,1)S(1)}, u32[]{:S(2)}, u32[]{:S(2)}) collective-permute-start(bf16[256,4096]{1,0:T(8,128)(2,1)S(1)} %bitcast.87), channel_id=1, source_target_pairs={{0,32},{32,64},{64,96},{96,0},{1,33},{33,65},{65,97},{97,1},{2,34}... | collective-permute-start | bytes 6291464 | tf_op jit(solution)/shard_map/ppermute | solution.py:28
  121.3 46.8 %collective-permute-start.5 = (bf16[256,4096]{1,0:T(8,128)(2,1)S(1)}, bf16[256,4096]{1,0:T(8,128)(2,1)S(1)}, u32[]{:S(2)}, u32[]{:S(2)}) collective-permute-start(bf16[256,4096]{1,0:T(8,128)(2,1)S(1)} %bitcast.88), channel_id=1, source_target_pairs={{0,96},{32,0},{64,32},{96,64},{1,97},{33,1},{65,33},{97,65},{2,98}... | collective-permute-start | bytes 6291464 | tf_op jit(solution)/shard_map/ppermute | solution.py:28
  140.9 113.2 %copy-start.2 = (bf16[1024,4096]{1,0:T(8,128)(2,1)}, bf16[1024,4096]{1,0:T(8,128)(2,1)S(1)}, u32[]{:S(2)}) copy-start(bf16[1024,4096]{1,0:T(8,128)(2,1)S(1)} %convolution_convert_fusion) | copy-start | bytes 25165828
  167.9 23.1 %collective-permute-start.6 = (bf16[128,4096]{1,0:T(8,128)(2,1)S(1)}, bf16[128,4096]{1,0:T(8,128)(2,1)S(1)}, u32[]{:S(2)}, u32[]{:S(2)}) collective-permute-start(bf16[128,4096]{1,0:T(8,128)(2,1)S(1)} %slice.125), channel_id=1, source_target_pairs={{0,32},{32,64},{64,96},{96,0},{1,33},{33,65},{65,97},{97,1},{2,34}... | collective-permute-start | bytes 3145736 | tf_op jit(solution)/shard_map/ppermute | solution.py:28
  168.2 22.9 %collective-permute-start.7 = (bf16[128,4096]{1,0:T(8,128)(2,1)S(1)}, bf16[128,4096]{1,0:T(8,128)(2,1)S(1)}, u32[]{:S(2)}, u32[]{:S(2)}) collective-permute-start(bf16[128,4096]{1,0:T(8,128)(2,1)S(1)} %slice.126), channel_id=1, source_target_pairs={{0,96},{32,0},{64,32},{96,64},{1,97},{33,1},{65,33},{97,65},{2,98}... | collective-permute-start | bytes 3145736 | tf_op jit(solution)/shard_map/ppermute | solution.py:28
  207.2 21.3 %collective-permute-start.12 = (bf16[128,4096]{1,0:T(8,128)(2,1)S(1)}, bf16[128,4096]{1,0:T(8,128)(2,1)S(1)}, u32[]{:S(2)}, u32[]{:S(2)}) collective-permute-start(bf16[128,4096]{1,0:T(8,128)(2,1)S(1)} %get-tuple-element.16), channel_id=1, source_target_pairs={{0,96},{32,0},{64,32},{96,64},{1,97},{33,1},{65,33},{97,65},{2,98}... | collective-permute-start | bytes 3145736 | tf_op jit(solution)/shard_map/ppermute | solution.py:28
  210.1 21.6 %collective-permute-start.14 = (bf16[128,4096]{1,0:T(8,128)(2,1)S(1)}, bf16[128,4096]{1,0:T(8,128)(2,1)S(1)}, u32[]{:S(2)}, u32[]{:S(2)}) collective-permute-start(bf16[128,4096]{1,0:T(8,128)(2,1)S(1)} %get-tuple-element.17), channel_id=1, source_target_pairs={{0,32},{32,64},{64,96},{96,0},{1,33},{33,65},{65,97},{97,1},{2,34}... | collective-permute-start | bytes 3145736 | tf_op jit(solution)/shard_map/ppermute | solution.py:28
  210.3 43.8 %collective-permute-start.10 = (bf16[128,4096]{1,0:T(8,128)(2,1)S(1)}, bf16[128,4096]{1,0:T(8,128)(2,1)S(1)}, u32[]{:S(2)}, u32[]{:S(2)}) collective-permute-start(bf16[128,4096]{1,0:T(8,128)(2,1)S(1)} %get-tuple-element.23), channel_id=1, source_target_pairs={{0,32},{32,64},{64,96},{96,0},{1,33},{33,65},{65,97},{97,1},{2,34}... | collective-permute-start | bytes 3145736 | tf_op jit(solution)/shard_map/ppermute | solution.py:28
  210.4 43.7 %collective-permute-start.8 = (bf16[128,4096]{1,0:T(8,128)(2,1)S(1)}, bf16[128,4096]{1,0:T(8,128)(2,1)S(1)}, u32[]{:S(2)}, u32[]{:S(2)}) collective-permute-start(bf16[128,4096]{1,0:T(8,128)(2,1)S(1)} %get-tuple-element.22), channel_id=1, source_target_pairs={{0,96},{32,0},{64,32},{96,64},{1,97},{33,1},{65,33},{97,65},{2,98}... | collective-permute-start | bytes 3145736 | tf_op jit(solution)/shard_map/ppermute | solution.py:28
  232.6 63.4 %collective-permute-start.13 = (bf16[256,4096]{1,0:T(8,128)(2,1)S(1)}, bf16[256,4096]{1,0:T(8,128)(2,1)S(1)}, u32[]{:S(2)}, u32[]{:S(2)}) collective-permute-start(bf16[256,4096]{1,0:T(8,128)(2,1)S(1)} %pad_maximum_fusion.2), channel_id=1, source_target_pairs={{0,96},{32,0},{64,32},{96,64},{1,97},{33,1},{65,33},{97,65},{2,98}... | collective-permute-start | bytes 6291464 | tf_op jit(solution)/shard_map/ppermute | solution.py:28
  233.1 65.9 %collective-permute-start.15 = (bf16[256,4096]{1,0:T(8,128)(2,1)S(1)}, bf16[256,4096]{1,0:T(8,128)(2,1)S(1)}, u32[]{:S(2)}, u32[]{:S(2)}) collective-permute-start(bf16[256,4096]{1,0:T(8,128)(2,1)S(1)} %pad_maximum_fusion.3), channel_id=1, source_target_pairs={{0,32},{32,64},{64,96},{96,0},{1,33},{33,65},{65,97},{97,1},{2,34}... | collective-permute-start | bytes 6291464 | tf_op jit(solution)/shard_map/ppermute | solution.py:28
  256.3 84.6 %collective-permute-start.9 = (bf16[256,4096]{1,0:T(8,128)(2,1)}, bf16[256,4096]{1,0:T(8,128)(2,1)}, u32[]{:S(2)}, u32[]{:S(2)}) collective-permute-start(bf16[256,4096]{1,0:T(8,128)(2,1)} %pad_maximum_fusion), channel_id=1, source_target_pairs={{0,96},{32,0},{64,32},{96,64},{1,97},{33,1},{65,33},{97,65},{2,98}... | collective-permute-start | bytes 6291464 | tf_op jit(solution)/shard_map/ppermute | solution.py:28
  258.2 85.9 %collective-permute-start.11 = (bf16[256,4096]{1,0:T(8,128)(2,1)}, bf16[256,4096]{1,0:T(8,128)(2,1)}, u32[]{:S(2)}, u32[]{:S(2)}) collective-permute-start(bf16[256,4096]{1,0:T(8,128)(2,1)} %pad_maximum_fusion.1), channel_id=1, source_target_pairs={{0,32},{32,64},{64,96},{96,0},{1,33},{33,65},{65,97},{97,1},{2,34}... | collective-permute-start | bytes 6291464 | tf_op jit(solution)/shard_map/ppermute | solution.py:28
  301.5 47.9 %all-to-all-start.3 = ((bf16[32,8,4096]{2,1,0:T(8,128)(2,1)}), bf16[32,8,4096]{2,1,0:T(8,128)(2,1)S(1)}, u32[]{:S(2)}, u32[]{:S(2)}) async-start(bf16[32,8,4096]{2,1,0:T(8,128)(2,1)} %fusion.16), calls=%async_computation.3 | async-start | bytes 4194304 | tf_op jit(solution)/shard_map/all_to_all | solution.py:68
  349.4 38.1 %all-to-all-start.2 = ((bf16[32,8,4096]{2,1,0:T(8,128)(2,1)}), bf16[32,8,4096]{2,1,0:T(8,128)(2,1)}, u32[]{:S(2)}, u32[]{:S(2)}) async-start(bf16[32,8,4096]{2,1,0:T(8,128)(2,1)} %fusion.15), calls=%async_computation.2 | async-start | bytes 4194304 | tf_op jit(solution)/shard_map/all_to_all | solution.py:68
  359.2 32.4 %copy-start.1 = (bf16[128,4096]{1,0:T(8,128)(2,1)S(1)}, bf16[128,4096]{1,0:T(8,128)(2,1)}, u32[]{:S(2)}) copy-start(bf16[128,4096]{1,0:T(8,128)(2,1)} %param.5) | copy-start | bytes 3145732
